TPU v7x, 128 devices: a whole 4x4x4 slice. The times are simulated.
128 devices in a mesh: chan: 8 (over x, core), tm: 16 (over z, y).
Axes of the slice: x: 4, y: 4, z: 4, core: 2. Of those that a mesh axis runs over, the one named last changes fastest.
Arguments:
- voltages: bfloat16 [128, 8192, 2, 512], P('tm', 'chan'), may hold values from -8 to 8
- window_stations: int32 [2], replicated, may hold values from 0 to 255
- channel_flags: int32 [8192], replicated, may hold values 0 or 1
Outputs:
- rm_spectrum: float32 [16, 16, 2, 2, 1024], P('tm', 'chan')
- leakage: float32 [2, 256], replicated
All inputs are finite; a program needn't handle non-finite values.
Results may differ from a plain program's by a relative error of at most 0.012.
Values may be sent and summed in bfloat16 or wider, within the bound.
No kernel may reach another device: no remote copies, remote signals or barrier semaphores. Data moves between devices by JAX's collectives and lax.ppermute only.
A program may use at most 128 MiB of HBM per device.

v0:
```python
import math

import jax
import jax.numpy as jnp
from jax import lax
from jax.sharding import PartitionSpec as P

CHANNELS = 8192
DEPTH = 1024
ITERATIONS = 3


def phase_table(first_channel, channel_count):
    chan_pos = (first_channel + jnp.arange(channel_count, dtype=jnp.int32)).astype(jnp.float32)
    frequency = 1.0 + (chan_pos + 0.5) / CHANNELS
    lambda_sq = 1.0 / (frequency * frequency)
    depth_grid = (jnp.arange(DEPTH).astype(jnp.float32) - DEPTH // 2) * 2.0
    angles = 2.0 * depth_grid[None, :] * (lambda_sq[:, None] - 0.5)
    return (jnp.cos(angles).astype(jnp.bfloat16), jnp.sin(angles).astype(jnp.bfloat16))


def station_terms(leak_real, leak_imag, fields, station_map, window_map):
    far_real = jnp.sum(station_map * leak_real[None, :], 1)[:, None]
    far_imag = jnp.sum(station_map * leak_imag[None, :], 1)[:, None]
    near_real = jnp.sum(window_map * leak_real[None, :], 1)[None, :]
    near_imag = jnp.sum(window_map * leak_imag[None, :], 1)[None, :]
    row_real = fields[0] - (far_real * fields[2] + far_imag * fields[3])
    row_imag = fields[1] - (far_real * fields[3] - far_imag * fields[2])
    col_real = fields[4] - (near_real * fields[2] + near_imag * fields[3])
    col_imag = -(fields[5] - (near_imag * fields[2] - near_real * fields[3]))
    numer_real = jnp.sum(window_map * jnp.sum(row_real, 0)[:, None], 0) + jnp.sum(
        station_map * jnp.sum(col_real, 1)[:, None], 0
    )
    numer_imag = jnp.sum(window_map * jnp.sum(row_imag, 0)[:, None], 0) + jnp.sum(
        station_map * jnp.sum(col_imag, 1)[:, None], 0
    )
    weight_sum = jnp.sum(window_map * jnp.sum(fields[6], 0)[:, None], 0) + jnp.sum(
        station_map * jnp.sum(fields[7], 1)[:, None], 0
    )
    return (numer_real, numer_imag, weight_sum)


def spectrum_terms(local_vis, first_channel, flag_weights):
    pairs = local_vis.shape[0] // 2
    window = local_vis.shape[2] // 2
    channel_count = local_vis.shape[3]
    six = local_vis.reshape(pairs, 2, 2, window, 2, channel_count)

    def correlation(feed_a, feed_b):
        return six[:, feed_b, :, :, feed_a, :].astype(jnp.float32)

    corr_xx = correlation(0, 0)
    corr_xy = correlation(0, 1)
    corr_yx = correlation(1, 0)
    corr_yy = correlation(1, 1)
    pol_real = 0.5 * (corr_xx[:, 0] - corr_yy[:, 0]) - 0.5 * (corr_xy[:, 1] + corr_yx[:, 1])
    pol_imag = 0.5 * (corr_xx[:, 1] - corr_yy[:, 1]) + 0.5 * (corr_xy[:, 0] + corr_yx[:, 0])
    pol_real = (pol_real * flag_weights).astype(jnp.bfloat16).reshape(pairs * window, channel_count)
    pol_imag = (pol_imag * flag_weights).astype(jnp.bfloat16).reshape(pairs * window, channel_count)

    def conj_sum(left, right):
        real_part = jnp.sum(
            flag_weights * (left[:, 0] * right[:, 0] + left[:, 1] * right[:, 1]), -1
        )
        imag_part = jnp.sum(
            flag_weights * (left[:, 1] * right[:, 0] - left[:, 0] * right[:, 1]), -1
        )
        return (real_part, imag_part)

    cross_real, cross_imag = conj_sum(corr_xy, corr_yy)
    mixed_real, mixed_imag = conj_sum(corr_xx, corr_yy)
    side_real, side_imag = conj_sum(corr_xy, corr_xx)
    power_y = jnp.sum(
        flag_weights * (corr_yy[:, 0] * corr_yy[:, 0] + corr_yy[:, 1] * corr_yy[:, 1]), -1
    )
    power_x = jnp.sum(
        flag_weights * (corr_xx[:, 0] * corr_xx[:, 0] + corr_xx[:, 1] * corr_xx[:, 1]), -1
    )
    baseline_stats = jnp.stack(
        [cross_real, cross_imag, mixed_real, mixed_imag, side_real, side_imag, power_y, power_x], -1
    )
    block_width = math.gcd(channel_count, 1024)

    def add_block(block_id, total):
        offset = block_id * block_width
        cosine, sine_part = phase_table(first_channel + offset, block_width)
        left = jnp.concatenate(
            [
                lax.dynamic_slice_in_dim(pol_real, offset, block_width, 1),
                lax.dynamic_slice_in_dim(pol_imag, offset, block_width, 1),
            ],
            1,
        )
        right = jnp.concatenate(
            [jnp.concatenate([cosine, -sine_part], 1), jnp.concatenate([sine_part, cosine], 1)], 0
        )
        return total + jnp.dot(left, right, preferred_element_type=jnp.float32)

    total = lax.fori_loop(
        0,
        channel_count // block_width,
        add_block,
        jnp.zeros((pairs * window, 2 * DEPTH), jnp.float32),
    )
    return (total.reshape(pairs, window, 2 * DEPTH), baseline_stats)


def per_device(voltages, window_stations, channel_flags):
    tm_size = lax.axis_size("tm")
    inputs = voltages.shape[3]
    stations = inputs // 2
    window = window_stations.shape[0]
    feed_index = (2 * window_stations[:, None] + jnp.arange(2, dtype=jnp.int32)[None, :]).reshape(
        -1
    )
    picked = jnp.take(voltages, feed_index, axis=3)
    blocks = jnp.einsum("tcaw,tcbx->xbawc", picked, voltages, preferred_element_type=jnp.float32)
    summed = lax.psum_scatter(
        jnp.stack([blocks[:, 0, 0] + blocks[:, 1, 1], blocks[:, 0, 1] - blocks[:, 1, 0]], 1).astype(
            jnp.bfloat16
        ),
        "tm",
        scatter_dimension=0,
        tiled=True,
    )
    chan_index = lax.axis_index("chan")
    relaid = lax.all_to_all(summed, "chan", split_axis=0, concat_axis=3, tiled=True)
    spectrum, baseline_stats = spectrum_terms(relaid, 0, channel_flags.astype(jnp.float32))
    own_pairs = spectrum.shape[0]
    total_time = voltages.shape[0] * tm_size
    norm_factor = 1.0 / math.sqrt(CHANNELS * total_time)
    rm_spectrum = (spectrum * norm_factor).reshape(1, own_pairs, window, 2, DEPTH)
    baseline_stats = baseline_stats / CHANNELS
    station_axis = jnp.arange(stations, dtype=jnp.int32)
    window_map = (window_stations[:, None] == station_axis[None, :]).astype(jnp.float32)
    leak_real = jnp.zeros((stations,), jnp.float32)
    leak_imag = jnp.zeros((stations,), jnp.float32)
    first_station = lax.axis_index("tm") * (stations // tm_size) + chan_index * own_pairs
    own_stations = first_station + jnp.arange(own_pairs, dtype=jnp.int32)
    station_map = (own_stations[:, None] == station_axis[None, :]).astype(jnp.float32)
    fields = [baseline_stats[:, :, column] for column in range(8)]
    for iteration in range(ITERATIONS):
        numer_real, numer_imag, weight_sum = station_terms(
            leak_real, leak_imag, fields, station_map, window_map
        )
        numer_real, numer_imag, weight_sum = lax.psum(
            (numer_real, numer_imag, weight_sum), ("chan", "tm")
        )
        leak_real = numer_real / (weight_sum + 1e-06)
        leak_imag = numer_imag / (weight_sum + 1e-06)
    return (rm_spectrum, jnp.stack([leak_real, leak_imag], 0))


def solution(mesh):
    return jax.shard_map(
        per_device,
        mesh=mesh,
        in_specs=(P("tm", "chan", None, None), P(), P()),
        out_specs=(P("tm", "chan", None, None, None), P()),
        check_vma=False,
    )
```

profile of v0, /device:TPU:0, one launch (start us, length us, event | category | flops | bytes accessed | tf_op | source)
XLA Modules:
  0.0 830.1 jit_solution(8393900596384874430)
XLA Ops:
  8.1 29.7 %copy.82 = bf16[8,1024,2,512]{1,0,2,3:T(8,128)(2,1)} copy(bf16[8,1024,2,512]{3,2,1,0:T(2,128)(2,1)} %param.5) | data formatting | bytes 33554432 | tf_op args[0]
  45.6 23.3 %fusion.20 = f32[512,2,2,4,1024]{0,3,1,2,4:T(4,128)} fusion(bf16[8,1024,2,4,1]{0,3,4,2,1:T(4,128)(2,1)S(1)} %copy.109, bf16[8,1024,2,512,1]{3,2,1,0,4:T(2,128)(2,1)} %bitcast.133), kind=kOutput, calls=%fused_computation.25 | convolution fusion | flops 134217728 | bytes 50462720 | tf_op jit(solution)/shard_map/tcaw,tcbx->xbawc/dot_general | solution.py:117
  90.5 18.8 %copy.87 = bf16[512,2,4,1024]{3,2,1,0:T(4,128)(2,1)} copy(bf16[512,2,4,1024]{0,2,3,1:T(4,128)(2,1)} %pad_maximum_fusion) | data formatting | bytes 16777216 | tf_op jit(solution)/shard_map/stack | solution.py:119
  111.3 142.8 %all-reduce.6.cloned.1.call-done = bf16[512,2,4,1024]{3,2,1,0:T(4,128)(2,1)} async-done(((bf16[512,2,4,1024]{3,2,1,0:T(4,128)(2,1)}), bf16[512,2,4,1024]{3,2,1,0:T(4,128)(2,1)}) %all-reduce.6.cloned.1.call-update) | async-done | bytes 8388624
  276.3 62.9 %all-reduce.3 = (f32[256]{0:T(256)S(1)}, f32[256]{0:T(256)S(1)}, f32[256]{0:T(256)S(1)}) all-reduce(f32[256]{0:T(256)S(1)} %add.318, f32[256]{0:T(256)S(1)} %add.316, f32[256]{0:T(256)S(1)} %add.315), channel_id=1, replica_groups=mesh['chan'=8,'tm'=16] {'chan','tm'}, use_global_device_ids=true, to_apply=%region_26.27 | all-reduce | flops 768 | bytes 6144 | tf_op jit(solution)/shard_map/psum | solution.py:146
  339.8 64.0 %all-reduce.2 = (f32[256]{0:T(256)S(1)}, f32[256]{0:T(256)S(1)}) all-reduce(f32[256]{0:T(256)S(1)} %add.322, f32[256]{0:T(256)S(1)} %add.321), channel_id=1, replica_groups=mesh['chan'=8,'tm'=16] {'chan','tm'}, use_global_device_ids=true, to_apply=%region_40.41 | all-reduce | flops 512 | bytes 4096 | tf_op jit(solution)/shard_map/psum | solution.py:146
  404.5 354.9 %while.16 = (s32[]{:T(128)}, f32[4,2048]{1,0:T(4,128)S(1)}, bf16[4,8192]{1,0:T(4,128)(2,1)S(1)}, bf16[4,8192]{1,0:T(4,128)(2,1)S(1)}, s32[]{:T(128)}, /*index=5*/s32[]{:T(128)}, s32[]{:T(128)}, s32[]{:T(128)}) while((s32[]{:T(128)}, f32[4,2048]{1,0:T(4,128)S(1)}, bf16[4,8192]{1,0:T(4,128)(2,1)S(1)}, bf16[4,8192]{1,0:T(4,128)(2,1)S(1)}, ...), condition=%wide.region_2.3_spmd.clone, body=%wide.region_1.2_spmd.clone.sunk | while | flops 75557896 | bytes 12722325 | solution.py:99
  404.6 16.9 %fusion.62 = (bf16[1024,1024]{1,0:T(8,128)(2,1)S(1)}, bf16[1024,1024]{1,0:T(8,128)(2,1)}) fusion(f32[1024]{0:T(1024)S(1)} %get-tuple-element.258, f32[1024]{0:T(1024)S(1)} %get-tuple-element.259), kind=kLoop, calls=%fused_computation.12.clone.2 | loop fusion | flops 3145728 | bytes 4202496 | tf_op jit(solution)/shard_map/while/body/eval_jaxpr/convert_element_type | solution.py:19
  421.5 15.1 %fusion.63 = bf16[1024,1024]{1,0:T(8,128)(2,1)} fusion(f32[1024]{0:T(1024)S(1)} %get-tuple-element.258, f32[1024]{0:T(1024)S(1)} %get-tuple-element.259), kind=kLoop, calls=%fused_computation.14.clone.1 | loop fusion | flops 5242880 | bytes 2105344 | tf_op jit(solution)/shard_map/while/body/eval_jaxpr/neg | solution.py:95
  449.0 16.9 %fusion.62 = (bf16[1024,1024]{1,0:T(8,128)(2,1)S(1)}, bf16[1024,1024]{1,0:T(8,128)(2,1)}) fusion(f32[1024]{0:T(1024)S(1)} %get-tuple-element.258, f32[1024]{0:T(1024)S(1)} %get-tuple-element.259), kind=kLoop, calls=%fused_computation.12.clone.2 | loop fusion | flops 3145728 | bytes 4202496 | tf_op jit(solution)/shard_map/while/body/eval_jaxpr/convert_element_type | solution.py:19
  465.9 15.1 %fusion.63 = bf16[1024,1024]{1,0:T(8,128)(2,1)} fusion(f32[1024]{0:T(1024)S(1)} %get-tuple-element.258, f32[1024]{0:T(1024)S(1)} %get-tuple-element.259), kind=kLoop, calls=%fused_computation.14.clone.1 | loop fusion | flops 5242880 | bytes 2105344 | tf_op jit(solution)/shard_map/while/body/eval_jaxpr/neg | solution.py:95
  493.3 16.9 %fusion.62 = (bf16[1024,1024]{1,0:T(8,128)(2,1)S(1)}, bf16[1024,1024]{1,0:T(8,128)(2,1)}) fusion(f32[1024]{0:T(1024)S(1)} %get-tuple-element.258, f32[1024]{0:T(1024)S(1)} %get-tuple-element.259), kind=kLoop, calls=%fused_computation.12.clone.2 | loop fusion | flops 3145728 | bytes 4202496 | tf_op jit(solution)/shard_map/while/body/eval_jaxpr/convert_element_type | solution.py:19
  510.2 15.1 %fusion.63 = bf16[1024,1024]{1,0:T(8,128)(2,1)} fusion(f32[1024]{0:T(1024)S(1)} %get-tuple-element.258, f32[1024]{0:T(1024)S(1)} %get-tuple-element.259), kind=kLoop, calls=%fused_computation.14.clone.1 | loop fusion | flops 5242880 | bytes 2105344 | tf_op jit(solution)/shard_map/while/body/eval_jaxpr/neg | solution.py:95
  537.7 16.9 %fusion.62 = (bf16[1024,1024]{1,0:T(8,128)(2,1)S(1)}, bf16[1024,1024]{1,0:T(8,128)(2,1)}) fusion(f32[1024]{0:T(1024)S(1)} %get-tuple-element.258, f32[1024]{0:T(1024)S(1)} %get-tuple-element.259), kind=kLoop, calls=%fused_computation.12.clone.2 | loop fusion | flops 3145728 | bytes 4202496 | tf_op jit(solution)/shard_map/while/body/eval_jaxpr/convert_element_type | solution.py:19
  554.6 15.1 %fusion.63 = bf16[1024,1024]{1,0:T(8,128)(2,1)} fusion(f32[1024]{0:T(1024)S(1)} %get-tuple-element.258, f32[1024]{0:T(1024)S(1)} %get-tuple-element.259), kind=kLoop, calls=%fused_computation.14.clone.1 | loop fusion | flops 5242880 | bytes 2105344 | tf_op jit(solution)/shard_map/while/body/eval_jaxpr/neg | solution.py:95
  582.0 16.9 %fusion.62 = (bf16[1024,1024]{1,0:T(8,128)(2,1)S(1)}, bf16[1024,1024]{1,0:T(8,128)(2,1)}) fusion(f32[1024]{0:T(1024)S(1)} %get-tuple-element.258, f32[1024]{0:T(1024)S(1)} %get-tuple-element.259), kind=kLoop, calls=%fused_computation.12.clone.2 | loop fusion | flops 3145728 | bytes 4202496 | tf_op jit(solution)/shard_map/while/body/eval_jaxpr/convert_element_type | solution.py:19
  598.9 15.1 %fusion.63 = bf16[1024,1024]{1,0:T(8,128)(2,1)} fusion(f32[1024]{0:T(1024)S(1)} %get-tuple-element.258, f32[1024]{0:T(1024)S(1)} %get-tuple-element.259), kind=kLoop, calls=%fused_computation.14.clone.1 | loop fusion | flops 5242880 | bytes 2105344 | tf_op jit(solution)/shard_map/while/body/eval_jaxpr/neg | solution.py:95
  626.4 16.9 %fusion.62 = (bf16[1024,1024]{1,0:T(8,128)(2,1)S(1)}, bf16[1024,1024]{1,0:T(8,128)(2,1)}) fusion(f32[1024]{0:T(1024)S(1)} %get-tuple-element.258, f32[1024]{0:T(1024)S(1)} %get-tuple-element.259), kind=kLoop, calls=%fused_computation.12.clone.2 | loop fusion | flops 3145728 | bytes 4202496 | tf_op jit(solution)/shard_map/while/body/eval_jaxpr/convert_element_type | solution.py:19
  643.3 15.1 %fusion.63 = bf16[1024,1024]{1,0:T(8,128)(2,1)} fusion(f32[1024]{0:T(1024)S(1)} %get-tuple-element.258, f32[1024]{0:T(1024)S(1)} %get-tuple-element.259), kind=kLoop, calls=%fused_computation.14.clone.1 | loop fusion | flops 5242880 | bytes 2105344 | tf_op jit(solution)/shard_map/while/body/eval_jaxpr/neg | solution.py:95
  670.7 16.9 %fusion.62 = (bf16[1024,1024]{1,0:T(8,128)(2,1)S(1)}, bf16[1024,1024]{1,0:T(8,128)(2,1)}) fusion(f32[1024]{0:T(1024)S(1)} %get-tuple-element.258, f32[1024]{0:T(1024)S(1)} %get-tuple-element.259), kind=kLoop, calls=%fused_computation.12.clone.2 | loop fusion | flops 3145728 | bytes 4202496 | tf_op jit(solution)/shard_map/while/body/eval_jaxpr/convert_element_type | solution.py:19
  687.7 15.1 %fusion.63 = bf16[1024,1024]{1,0:T(8,128)(2,1)} fusion(f32[1024]{0:T(1024)S(1)} %get-tuple-element.258, f32[1024]{0:T(1024)S(1)} %get-tuple-element.259), kind=kLoop, calls=%fused_computation.14.clone.1 | loop fusion | flops 5242880 | bytes 2105344 | tf_op jit(solution)/shard_map/while/body/eval_jaxpr/neg | solution.py:95
  715.1 16.9 %fusion.62 = (bf16[1024,1024]{1,0:T(8,128)(2,1)S(1)}, bf16[1024,1024]{1,0:T(8,128)(2,1)}) fusion(f32[1024]{0:T(1024)S(1)} %get-tuple-element.258, f32[1024]{0:T(1024)S(1)} %get-tuple-element.259), kind=kLoop, calls=%fused_computation.12.clone.2 | loop fusion | flops 3145728 | bytes 4202496 | tf_op jit(solution)/shard_map/while/body/eval_jaxpr/convert_element_type | solution.py:19
  732.0 15.1 %fusion.63 = bf16[1024,1024]{1,0:T(8,128)(2,1)} fusion(f32[1024]{0:T(1024)S(1)} %get-tuple-element.258, f32[1024]{0:T(1024)S(1)} %get-tuple-element.259), kind=kLoop, calls=%fused_computation.14.clone.1 | loop fusion | flops 5242880 | bytes 2105344 | tf_op jit(solution)/shard_map/while/body/eval_jaxpr/neg | solution.py:95
  760.3 62.4 %all-reduce.1 = (f32[256]{0:T(256)S(1)}, f32[256]{0:T(256)S(1)}) all-reduce(f32[256]{0:T(256)S(1)} %add.326, f32[256]{0:T(256)S(1)} %add.325), channel_id=1, replica_groups=mesh['chan'=8,'tm'=16] {'chan','tm'}, use_global_device_ids=true, to_apply=%region_53.54 | all-reduce | flops 512 | bytes 4096 | tf_op jit(solution)/shard_map/psum | solution.py:146
  (104 shorter events, 155.1 us)
Async XLA Ops:
  7.2 246.9 %all-reduce.6.cloned.1.call-start = ((), (), s32[]{:S(2)}) async-start(), calls=%async_computation.1 | async-start | bytes 16777216
  109.4 0.7 copy-start.2
  109.4 151.0 %copy-start = (s32[8192]{0:T(1024)S(1)}, s32[8192]{0:T(1024)}, u32[]{:S(2)}) copy-start(s32[8192]{0:T(1024)} %param.7) | copy-start | bytes 98308
  109.4 166.7 %copy-start.1 = (s32[2]{0:T(128)S(1)}, s32[2]{0:T(128)}, u32[]{:S(2)}) copy-start(s32[2]{0:T(128)} %param.6) | copy-start | bytes 28
  256.1 14.6 %all-to-all-start = ((bf16[32,2,4,1024]{3,2,1,0:T(4,128)(2,1)}), bf16[32,2,4,1024]{3,2,1,0:T(4,128)(2,1)S(1)}, u32[]{:S(2)}, u32[]{:S(2)}) async-start(bf16[32,2,4,1024]{3,2,1,0:T(4,128)(2,1)} %constant_dynamic-slice_fusion.2), calls=%async_computation | async-start | bytes 1048576 | tf_op jit(solution)/shard_map/all_to_all | solution.py:127
Sparse Core Ops, SparseCore 0:
  109.5 144.4 all-reduce.5
where the time goes:
time: 833 us; the launch traced here: 830 us
  other arithmetic  284 us (34%)
  blocking collectives  189 us (23%)
  waiting for transfers between devices  153 us (18%)
  matrix products  122 us (15%)
  local copies, waits for them, and re-layouts  62.4 us (7%)
  between operations  14.9 us (2%)
    psum x3, blocking collectives, per_device(): lax.psum((numer_real, numer_imag, weight_sum), ('chan', 'tm'))  189 us
    unnamed x2, waiting for transfers between devices  143 us
    convert_element_type x8, other arithmetic, phase_table(): jnp.sin(angles).astype(jnp.bfloat16)  135 us
    neg x8, other arithmetic, add_block(): -sine_part  121 us
    dot_general x8, matrix products, add_block(): return total + jnp.dot(left, right, preferred_element_type=jnp.float32)  98.5 us
    unnamed x10, local copies, waits for them, and re-layouts  33.2 us
    dot_general x1, matrix products, per_device(): jnp.einsum('tcaw,tcbx->xbawc', picked, voltages, preferred_element_type=j...  23.3 us
    another operation x1, local copies, waits for them, and re-layouts, per_device(): jnp.stack([blocks[:, 0, 0] + blocks[:, 1, 1], blocks[:, 0, 1] - blocks[:,...  18.8 us
  transfers between devices with their start and end apart: 2, of which 2 were waited for; matrix products, arithmetic and copies ran while one was open for 0% of the time, Pallas kernels for 0%

commit v1 on v0

--- a/solution.py
+++ b/solution.py
@@ -107,9 +107,11 @@
 
 def per_device(voltages, window_stations, channel_flags):
     tm_size = lax.axis_size("tm")
+    chan_size = lax.axis_size("chan")
     inputs = voltages.shape[3]
     stations = inputs // 2
     window = window_stations.shape[0]
+    channel_count = voltages.shape[1]
     feed_index = (2 * window_stations[:, None] + jnp.arange(2, dtype=jnp.int32)[None, :]).reshape(
         -1
     )
@@ -124,27 +126,34 @@
         tiled=True,
     )
     chan_index = lax.axis_index("chan")
-    relaid = lax.all_to_all(summed, "chan", split_axis=0, concat_axis=3, tiled=True)
-    spectrum, baseline_stats = spectrum_terms(relaid, 0, channel_flags.astype(jnp.float32))
-    own_pairs = spectrum.shape[0]
+    tm_index = lax.axis_index("tm")
+    first_channel = chan_index * channel_count
+    local_flags = lax.dynamic_slice_in_dim(channel_flags, first_channel, channel_count, 0)
+    spectrum, baseline_stats = spectrum_terms(
+        summed, first_channel, local_flags.astype(jnp.float32)
+    )
+    block_pairs = spectrum.shape[0]
     total_time = voltages.shape[0] * tm_size
     norm_factor = 1.0 / math.sqrt(CHANNELS * total_time)
+    spectrum = lax.psum_scatter(spectrum, "chan", scatter_dimension=0, tiled=True)
+    own_pairs = spectrum.shape[0]
     rm_spectrum = (spectrum * norm_factor).reshape(1, own_pairs, window, 2, DEPTH)
-    baseline_stats = baseline_stats / CHANNELS
+    all_stats = lax.dynamic_update_slice_in_dim(
+        jnp.zeros((stations, window, 8), jnp.float32),
+        baseline_stats,
+        tm_index * block_pairs,
+        0,
+    )
+    all_stats = lax.psum(all_stats, ("chan", "tm")) / CHANNELS
     station_axis = jnp.arange(stations, dtype=jnp.int32)
     window_map = (window_stations[:, None] == station_axis[None, :]).astype(jnp.float32)
+    station_map = jnp.eye(stations, dtype=jnp.float32)
     leak_real = jnp.zeros((stations,), jnp.float32)
     leak_imag = jnp.zeros((stations,), jnp.float32)
-    first_station = lax.axis_index("tm") * (stations // tm_size) + chan_index * own_pairs
-    own_stations = first_station + jnp.arange(own_pairs, dtype=jnp.int32)
-    station_map = (own_stations[:, None] == station_axis[None, :]).astype(jnp.float32)
-    fields = [baseline_stats[:, :, column] for column in range(8)]
+    fields = [all_stats[:, :, column] for column in range(8)]
     for iteration in range(ITERATIONS):
         numer_real, numer_imag, weight_sum = station_terms(
             leak_real, leak_imag, fields, station_map, window_map
-        )
-        numer_real, numer_imag, weight_sum = lax.psum(
-            (numer_real, numer_imag, weight_sum), ("chan", "tm")
         )
         leak_real = numer_real / (weight_sum + 1e-06)
         leak_imag = numer_imag / (weight_sum + 1e-06)

time: 833 us -> 405 us (0.49)
  other arithmetic: 284 us -> 59 us
  blocking collectives: 189 us -> 64.7 us
  matrix products: 122 us -> 35.7 us
  waiting for transfers between devices: 153 us -> 166 us
    psum x3 -> x1, blocking collectives: 189 us -> 64.7 us  [per_device(): all_stats = lax.psum(all_stats, ('chan', 'tm')) / CHANNELS]
    convert_element_type x8 -> x1, other arithmetic: 135 us -> 17 us  [phase_table(): jnp.sin(angles).astype(jnp.bfloat16)]
    neg x8 -> x1, other arithmetic: 121 us -> 14.4 us  [add_block(): -sine_part]
    dot_general x8 -> x1, matrix products: 98.5 us -> 12.4 us  [add_block(): return total + jnp.dot(left, right, preferred_element_type=jnp.float32)]
    unnamed x2 -> x4, waiting for transfers between devices: 143 us -> 166 us
    all_to_all x1 -> x0, waiting for transfers between devices: 10.3 us -> none  [per_device(): lax.all_to_all(summed, 'chan', split_axis=0, concat_axis=3, tiled=True)]
    unnamed x10 -> x17, local copies, waits for them, and re-layouts: 33.2 us -> 32.5 us
  transfers between devices with their start and end apart: 2 -> 2, of which waited for: 2 -> 2; matrix products, arithmetic and copies ran while one was open for 0% -> 8% of each run, Pallas kernels for 0% -> 0%
where the time goes in v1:
time: 405 us; the launch traced here: 403 us
  waiting for transfers between devices  166 us (41%)
  blocking collectives  64.7 us (16%)
  local copies, waits for them, and re-layouts  62.3 us (15%)
  other arithmetic  59 us (15%)
  matrix products  35.7 us (9%)
  between operations  15.6 us (4%)
    unnamed x4, waiting for transfers between devices  166 us
    psum x1, blocking collectives, per_device(): all_stats = lax.psum(all_stats, ('chan', 'tm')) / CHANNELS  64.7 us
    unnamed x17, local copies, waits for them, and re-layouts  32.5 us
    dot_general x1, matrix products, per_device(): jnp.einsum('tcaw,tcbx->xbawc', picked, voltages, preferred_element_type=j...  23.3 us
    another operation x1, local copies, waits for them, and re-layouts, per_device(): jnp.stack([blocks[:, 0, 0] + blocks[:, 1, 1], blocks[:, 0, 1] - blocks[:,...  18.8 us
    convert_element_type x1, other arithmetic, phase_table(): jnp.sin(angles).astype(jnp.bfloat16)  17 us
    neg x1, other arithmetic, add_block(): -sine_part  14.4 us
    dot_general x1, matrix products, add_block(): return total + jnp.dot(left, right, preferred_element_type=jnp.float32)  12.4 us
  transfers between devices with their start and end apart: 2, of which 2 were waited for; matrix products, arithmetic and copies ran while one was open for 8% of the time, Pallas kernels for 0%

profile of v1, /device:TPU:0, one launch (start us, length us, event | category | flops | bytes accessed | tf_op | source)
XLA Modules:
  0.0 403.4 jit_solution(6623652961401144350)
XLA Ops:
  7.2 0.7 broadcast_multiply_fusion.2
  8.1 29.7 %copy.84 = bf16[8,1024,2,512]{1,0,2,3:T(8,128)(2,1)} copy(bf16[8,1024,2,512]{3,2,1,0:T(2,128)(2,1)} %param.3) | data formatting | bytes 33554432 | tf_op args[0]
  37.8 6.3 %gather_fusion = bf16[4,8,1024,2]{2,1,3,0:T(8,128)(2,1)S(1)} fusion(bf16[8,1024,2,512]{1,0,2,3:T(8,128)(2,1)} %copy.84, s32[1024]{0:T(1024)S(1)} %pad_clamp_fusion), kind=kCustom, calls=%fused_computation | custom fusion | bytes 262160 | tf_op jit(solution)/shard_map/jit(_take)/gather | solution.py:118
  44.2 1.4 copy.113
  45.6 23.3 %fusion.2 = f32[512,2,2,4,1024]{0,3,1,2,4:T(4,128)} fusion(bf16[8,1024,2,4,1]{0,3,4,2,1:T(4,128)(2,1)S(1)} %copy.113, bf16[8,1024,2,512,1]{3,2,1,0,4:T(2,128)(2,1)} %bitcast.189), kind=kOutput, calls=%fused_computation.3 | convolution fusion | flops 134217728 | bytes 50462720 | tf_op jit(solution)/shard_map/tcaw,tcbx->xbawc/dot_general | solution.py:119
  68.9 7.1 %fusion.18 = bf16[512,1,4,1024]{0,2,3,1:T(4,128)(2,1)S(1)} fusion(f32[512,2,2,4,1024]{0,3,1,2,4:T(4,128)} %fusion.2), kind=kLoop, calls=%fused_computation.23 | loop fusion | flops 4194304 | bytes 20971520 | tf_op jit(solution)/shard_map/add | solution.py:121
  76.0 7.1 %fusion.19 = bf16[512,1,4,1024]{0,2,3,1:T(4,128)(2,1)S(1)} fusion(f32[512,2,2,4,1024]{0,3,1,2,4:T(4,128)} %fusion.2), kind=kLoop, calls=%fused_computation.24 | loop fusion | flops 4194304 | bytes 20971520 | tf_op jit(solution)/shard_map/sub | solution.py:121
  83.1 7.4 %pad_maximum_fusion = bf16[512,2,4,1024]{0,2,3,1:T(4,128)(2,1)} fusion(bf16[512,1,4,1024]{0,2,3,1:T(4,128)(2,1)S(1)} %fusion.19, bf16[512,1,4,1024]{0,2,3,1:T(4,128)(2,1)S(1)} %fusion.18), kind=kLoop, calls=%fused_computation.10 | loop fusion | flops 4194304 | bytes 16777216 | tf_op jit(solution)/shard_map/stack | solution.py:121
  90.5 18.8 %copy.89 = bf16[512,2,4,1024]{3,2,1,0:T(4,128)(2,1)} copy(bf16[512,2,4,1024]{0,2,3,1:T(4,128)(2,1)} %pad_maximum_fusion) | data formatting | bytes 16777216 | tf_op jit(solution)/shard_map/stack | solution.py:121
  110.0 0.6 dynamic-slice
  110.6 0.6 dynamic-slice.2
  112.5 0.7 broadcast_multiply_fusion.1
  113.2 14.4 %fusion.20 = bf16[1024,1024]{1,0:T(8,128)(2,1)S(1)} fusion(f32[1024]{0:T(1024)S(1)} %get-tuple-element.80, f32[1024]{0:T(1024)S(1)} %get-tuple-element.81), kind=kLoop, calls=%fused_computation.25 | loop fusion | flops 5242880 | bytes 2105344 | tf_op jit(solution)/shard_map/while/body/eval_jaxpr/neg | solution.py:95
  127.6 17.0 %fusion.17 = (bf16[1024,1024]{1,0:T(8,128)(2,1)}, bf16[1024,1024]{1,0:T(8,128)(2,1)}) fusion(f32[1024]{0:T(1024)S(1)} %get-tuple-element.80, f32[1024]{0:T(1024)S(1)} %get-tuple-element.81), kind=kLoop, calls=%fused_computation.22 | loop fusion | flops 3145728 | bytes 4202496 | tf_op jit(solution)/shard_map/while/body/eval_jaxpr/convert_element_type | solution.py:19
  144.6 109.4 %all-reduce.5.cloned.1.call-done = bf16[512,2,4,1024]{3,2,1,0:T(4,128)(2,1)} async-done(((bf16[512,2,4,1024]{3,2,1,0:T(4,128)(2,1)}), bf16[512,2,4,1024]{3,2,1,0:T(4,128)(2,1)}) %all-reduce.5.cloned.1.call-update) | async-done | bytes 8388624
  254.0 1.3 constant_dynamic-slice_fusion
  255.3 0.5 copy.90
  257.0 64.7 %psum.7 = f32[256,2,8]{0,1,2:T(2,128)S(1)} all-reduce(f32[256,2,8]{0,1,2:T(2,128)S(1)} %dynamic_update_slice.3), channel_id=1, replica_groups=mesh['chan'=8,'tm'=16] {'chan','tm'}, use_global_device_ids=true, to_apply=%region_10.11 | all-reduce | flops 4096 | bytes 32768 | tf_op jit(solution)/shard_map/psum | solution.py:147
  324.7 12.4 %fusion.8 = f32[32,2048]{1,0:T(8,128)S(1)} fusion(bf16[1024,1024]{1,0:T(8,128)(2,1)} %get-tuple-element.75, bf16[1024,1024]{1,0:T(8,128)(2,1)} %get-tuple-element.74, bf16[1024,1024]{1,0:T(8,128)(2,1)S(1)} %fusion.20, bf16[32,1024]{1,0:T(8,128)(2,1)S(1)} %multiply_convert_fusion, bf16[32,1024]{1,0:T(8,128)(2,1)S(1)} %multiply_convert_fusion.1), kind=kOutput, calls=%fused_computation.11 | convolution fusion | flops 302252032 | bytes 6684672 | tf_op jit(solution)/shard_map/while/body/eval_jaxpr/dot_general | solution.py:97
  337.1 0.8 reshape.293
  338.1 0.6 pad_maximum_fusion.1
  338.7 56.5 %all-reduce.7.cloned.1.call-done = f32[16,2,2048]{2,1,0:T(2,128)} async-done(((f32[16,2,2048]{2,1,0:T(2,128)}), f32[16,2,2048]{2,1,0:T(2,128)}) %all-reduce.7.cloned.1.call-update) | async-done | bytes 262160
  395.2 0.8 dynamic-slice_multiply_fusion
  395.9 0.7 reshape.294
  (68 shorter events, 5.2 us)
Async XLA Ops:
  7.2 246.9 %all-reduce.5.cloned.1.call-start = ((), (), s32[]{:S(2)}) async-start(), calls=%async_computation | async-start | bytes 16777216
  109.4 0.7 copy-start.2
  109.4 1.2 copy-start.1
  109.4 212.9 %copy-start = (s32[2]{0:T(128)S(1)}, s32[2]{0:T(128)}, u32[]{:S(2)}) copy-start(s32[2]{0:T(128)} %param.4) | copy-start | bytes 28
  109.4 285.7 %all-reduce.7.cloned.1.call-start = ((), (), s32[]{:S(2)}) async-start(), calls=%async_computation.1 | async-start | bytes 524288
Sparse Core Ops, SparseCore 0:
  109.5 144.4 all-reduce.4
  338.1 56.9 all-reduce.6

commit v2 on v1

--- a/solution.py
+++ b/solution.py
@@ -117,14 +117,16 @@
     )
     picked = jnp.take(voltages, feed_index, axis=3)
     blocks = jnp.einsum("tcaw,tcbx->xbawc", picked, voltages, preferred_element_type=jnp.float32)
+    partial = jnp.stack(
+        [blocks[:, 0, 0] + blocks[:, 1, 1], blocks[:, 0, 1] - blocks[:, 1, 0]], 1
+    ).astype(jnp.bfloat16)
+    partial_shape = partial.shape
     summed = lax.psum_scatter(
-        jnp.stack([blocks[:, 0, 0] + blocks[:, 1, 1], blocks[:, 0, 1] - blocks[:, 1, 0]], 1).astype(
-            jnp.bfloat16
-        ),
+        partial.reshape(partial_shape[0], -1, partial_shape[-1]),
         "tm",
         scatter_dimension=0,
         tiled=True,
-    )
+    ).reshape(-1, *partial_shape[1:])
     chan_index = lax.axis_index("chan")
     tm_index = lax.axis_index("tm")
     first_channel = chan_index * channel_count
@@ -135,8 +137,10 @@
     block_pairs = spectrum.shape[0]
     total_time = voltages.shape[0] * tm_size
     norm_factor = 1.0 / math.sqrt(CHANNELS * total_time)
-    spectrum = lax.psum_scatter(spectrum, "chan", scatter_dimension=0, tiled=True)
-    own_pairs = spectrum.shape[0]
+    spectrum = lax.psum_scatter(
+        spectrum.reshape(block_pairs // 2, -1, DEPTH), "chan", scatter_dimension=0, tiled=True
+    )
+    own_pairs = block_pairs // chan_size
     rm_spectrum = (spectrum * norm_factor).reshape(1, own_pairs, window, 2, DEPTH)
     all_stats = lax.dynamic_update_slice_in_dim(
         jnp.zeros((stations, window, 8), jnp.float32),
@@ -144,7 +148,7 @@
         tm_index * block_pairs,
         0,
     )
-    all_stats = lax.psum(all_stats, ("chan", "tm")) / CHANNELS
+    all_stats = lax.psum(all_stats.reshape(-1, 128), ("chan", "tm")).reshape(all_stats.shape) / CHANNELS
     station_axis = jnp.arange(stations, dtype=jnp.int32)
     window_map = (window_stations[:, None] == station_axis[None, :]).astype(jnp.float32)
     station_map = jnp.eye(stations, dtype=jnp.float32)

time: 405 us -> 328 us (0.81)
  waiting for transfers between devices: 166 us -> 82.6 us
  other arithmetic: 59 us -> 66.6 us
    unnamed x4 -> x2, waiting for transfers between devices: 166 us -> 0.03 us
    reduce_scatter x0 -> x2, waiting for transfers between devices: none -> 82.5 us  [the longest x1 56.2 us: per_device(): lax.psum_scatter(partial.reshape(partial_shape[0], -1, partial_shape[-1])...]
    slice x0 -> x6, local copies, waits for them, and re-layouts: none -> 5.46 us  [per_device(): fields = [all_stats[:, :, column] for column in range(8)]]
    another operation x1, local copies, waits for them, and re-layouts: 18.8 us -> 13.7 us  [per_device(): jnp.stack([blocks[:, 0, 0] + blocks[:, 1, 1], blocks[:, 0, 1] - blocks[:,...]
    reduce_sum x1, other arithmetic: 0.12 us -> 4.53 us  [station_terms(): jnp.sum(fields[7], 1)[:, None]]
    unnamed x17 -> x10, local copies, waits for them, and re-layouts: 32.5 us -> 29.7 us
  transfers between devices with their start and end apart: 2 -> 2, of which waited for: 2 -> 2; matrix products, arithmetic and copies ran while one was open for 8% -> 10% of each run, Pallas kernels for 0% -> 0%
where the time goes in v2:
time: 328 us; the launch traced here: 326 us
  waiting for transfers between devices  82.6 us (25%)
  other arithmetic  66.6 us (20%)
  blocking collectives  64.9 us (20%)
  local copies, waits for them, and re-layouts  62.1 us (19%)
  matrix products  35.7 us (11%)
  between operations  14.3 us (4%)
    psum x1, blocking collectives, per_device(): lax.psum(all_stats.reshape(-1, 128), ('chan', 'tm'))  64.9 us
    reduce_scatter x1, waiting for transfers between devices, per_device(): lax.psum_scatter(partial.reshape(partial_shape[0], -1, partial_shape[-1])...  56.2 us
    unnamed x10, local copies, waits for them, and re-layouts  29.7 us
    reduce_scatter x1, waiting for transfers between devices, per_device(): lax.psum_scatter(spectrum.reshape(block_pairs // 2, -1, DEPTH), 'chan', s...  26.3 us
    dot_general x1, matrix products, per_device(): jnp.einsum('tcaw,tcbx->xbawc', picked, voltages, preferred_element_type=j...  23.3 us
    convert_element_type x1, other arithmetic, phase_table(): jnp.sin(angles).astype(jnp.bfloat16)  17 us
    neg x1, other arithmetic, add_block(): -sine_part  14.4 us
    another operation x1, local copies, waits for them, and re-layouts, per_device(): jnp.stack([blocks[:, 0, 0] + blocks[:, 1, 1], blocks[:, 0, 1] - blocks[:,...  13.7 us
  transfers between devices with their start and end apart: 2, of which 2 were waited for; matrix products, arithmetic and copies ran while one was open for 10% of the time, Pallas kernels for 0%

profile of v2, /device:TPU:0, one launch (start us, length us, event | category | flops | bytes accessed | tf_op | source)
XLA Modules:
  0.0 326.3 jit_solution(1268956733887348137)
XLA Ops:
  8.1 29.7 %copy.198 = bf16[8,1024,2,512]{1,0,2,3:T(8,128)(2,1)} copy(bf16[8,1024,2,512]{3,2,1,0:T(2,128)(2,1)} %param.3) | data formatting | bytes 33554432 | tf_op args[0]
  37.8 6.3 %gather_fusion = bf16[4,8,1024,2]{2,1,3,0:T(8,128)(2,1)S(1)} fusion(bf16[8,1024,2,512]{1,0,2,3:T(8,128)(2,1)} %copy.198, s32[1024]{0:T(1024)S(1)} %pad_clamp_fusion), kind=kCustom, calls=%fused_computation | custom fusion | bytes 262160 | tf_op jit(solution)/shard_map/jit(_take)/gather | solution.py:118
  44.2 1.4 copy.223
  45.6 23.3 %fusion.2 = f32[512,2,2,4,1024]{0,3,1,2,4:T(4,128)} fusion(bf16[8,1024,2,4,1]{0,3,4,2,1:T(4,128)(2,1)S(1)} %copy.223, bf16[8,1024,2,512,1]{3,2,1,0,4:T(2,128)(2,1)} %bitcast.241), kind=kOutput, calls=%fused_computation.3 | convolution fusion | flops 134217728 | bytes 50462720 | tf_op jit(solution)/shard_map/tcaw,tcbx->xbawc/dot_general | solution.py:119
  68.9 7.1 %fusion.18 = bf16[512,1,4,1024]{0,2,3,1:T(4,128)(2,1)S(1)} fusion(f32[512,2,2,4,1024]{0,3,1,2,4:T(4,128)} %fusion.2), kind=kLoop, calls=%fused_computation.23 | loop fusion | flops 4194304 | bytes 20971520 | tf_op jit(solution)/shard_map/add | solution.py:121
  76.0 7.1 %fusion.19 = bf16[512,1,4,1024]{0,2,3,1:T(4,128)(2,1)S(1)} fusion(f32[512,2,2,4,1024]{0,3,1,2,4:T(4,128)} %fusion.2), kind=kLoop, calls=%fused_computation.24 | loop fusion | flops 4194304 | bytes 20971520 | tf_op jit(solution)/shard_map/sub | solution.py:121
  83.1 7.4 %pad_maximum_fusion = bf16[512,2,4,1024]{0,2,3,1:T(4,128)(2,1)} fusion(bf16[512,1,4,1024]{0,2,3,1:T(4,128)(2,1)S(1)} %fusion.19, bf16[512,1,4,1024]{0,2,3,1:T(4,128)(2,1)S(1)} %fusion.18), kind=kLoop, calls=%fused_computation.10 | loop fusion | flops 4194304 | bytes 16777216 | tf_op jit(solution)/shard_map/stack | solution.py:120
  90.5 13.7 %copy.203 = bf16[512,2,4,1024]{3,0,2,1:T(8,128)(2,1)} copy(bf16[512,2,4,1024]{0,2,3,1:T(4,128)(2,1)} %pad_maximum_fusion) | data formatting | bytes 16777216 | tf_op jit(solution)/shard_map/stack | solution.py:120
  105.2 14.4 %fusion.20 = bf16[1024,1024]{1,0:T(8,128)(2,1)S(1)} fusion(f32[1024]{0:T(1024)S(1)} %get-tuple-element.86, f32[1024]{0:T(1024)S(1)} %get-tuple-element.87), kind=kLoop, calls=%fused_computation.25 | loop fusion | flops 5242880 | bytes 2105344 | tf_op jit(solution)/shard_map/while/body/eval_jaxpr/neg | solution.py:95
  119.6 17.0 %fusion.17 = (bf16[1024,1024]{1,0:T(8,128)(2,1)}, bf16[1024,1024]{1,0:T(8,128)(2,1)}) fusion(f32[1024]{0:T(1024)S(1)} %get-tuple-element.86, f32[1024]{0:T(1024)S(1)} %get-tuple-element.87), kind=kLoop, calls=%fused_computation.22 | loop fusion | flops 3145728 | bytes 4202496 | tf_op jit(solution)/shard_map/while/body/eval_jaxpr/convert_element_type | solution.py:19
  136.7 56.2 %reduce-scatter.3.cloned.1.call-done = bf16[32,8,1024]{2,0,1:T(8,128)(2,1)} async-done(((bf16[512,8,1024]{2,0,1:T(8,128)(2,1)}), bf16[32,8,1024]{2,0,1:T(8,128)(2,1)}) %reduce-scatter.3.cloned.1.call-update) | async-done | bytes 524304 | tf_op jit(solution)/shard_map/reduce_scatter | solution.py:124
  192.8 1.2 reshape_reshape.6
  195.4 1.1 fusion.27
  196.5 1.0 fusion.33
  198.7 64.9 %psum.7 = f32[32,128]{1,0:T(8,128)S(1)} all-reduce(f32[32,128]{1,0:T(8,128)S(1)} %reshape.296), channel_id=1, replica_groups=mesh['chan'=8,'tm'=16] {'chan','tm'}, use_global_device_ids=true, to_apply=%region_10.11 | all-reduce | flops 4096 | bytes 32768 | tf_op jit(solution)/shard_map/psum | solution.py:151
  264.0 4.5 %slice_reduce_fusion = (f32[256]{0:T(256)S(1)}, f32[2]{0:T(128)S(1)}, f32[256,2,1]{2,1,0:T(2,128)}, f32[256,2,1]{2,1,0:T(2,128)S(1)}, f32[256,2,1]{2,1,0:T(2,128...) fusion(f32[256,2,8]{2,1,0:T(2,128)S(1)} %div.78), kind=kLoop, calls=%fused_computation.26 | loop fusion | flops 766 | bytes 29704 | tf_op jit(solution)/shard_map/reduce_sum | solution.py:38
  268.5 1.1 copy.217
  269.6 1.1 copy.218
  270.7 1.1 copy.219
  271.7 1.1 copy.220
  272.8 1.1 copy.221
  276.3 1.3 fusion.23
  277.8 12.4 %fusion.8 = f32[32,2048]{1,0:T(8,128)S(1)} fusion(bf16[1024,1024]{1,0:T(8,128)(2,1)} %get-tuple-element.81, bf16[1024,1024]{1,0:T(8,128)(2,1)} %get-tuple-element.80, bf16[1024,1024]{1,0:T(8,128)(2,1)S(1)} %fusion.20, bf16[32,1024]{1,0:T(8,128)(2,1)S(1)} %multiply_convert_fusion, bf16[32,1024]{1,0:T(8,128)(2,1)S(1)} %multiply_convert_fusion.1), kind=kOutput, calls=%fused_computation.11 | convolution fusion | flops 302252032 | bytes 6684672 | tf_op jit(solution)/shard_map/while/body/eval_jaxpr/dot_general | solution.py:97
  291.7 26.3 %reduce-scatter.5.cloned.1.call-done = f32[1,8,1024]{2,1,0:T(8,128)} async-done(((f32[8,8,1024]{2,1,0:T(8,128)}), f32[1,8,1024]{2,1,0:T(8,128)}) %reduce-scatter.5.cloned.1.call-update) | async-done | bytes 32784 | tf_op jit(solution)/shard_map/reduce_scatter | solution.py:140
  (75 shorter events, 10.4 us)
Async XLA Ops:
  7.2 185.7 %reduce-scatter.3.cloned.1.call-start = ((), (), s32[]{:S(2)}) async-start(), calls=%async_computation.2 | async-start | bytes 8912896 | tf_op jit(solution)/shard_map/reduce_scatter | solution.py:124
  104.3 213.8 %reduce-scatter.5.cloned.1.call-start = ((), (), s32[]{:S(2)}) async-start(), calls=%async_computation.3 | async-start | bytes 294912 | tf_op jit(solution)/shard_map/reduce_scatter | solution.py:140
  119.6 154.9 %copy-start = (s32[2]{0:T(128)S(1)}, s32[2]{0:T(128)}, u32[]{:S(2)}) copy-start(s32[2]{0:T(128)} %param.4) | copy-start | bytes 28
Sparse Core Ops, SparseCore 0:
  104.4 88.3 reduce-scatter.2
  291.0 26.9 reduce-scatter.4

commit v3 on v2

--- a/solution.py
+++ b/solution.py
@@ -142,13 +142,9 @@
     )
     own_pairs = block_pairs // chan_size
     rm_spectrum = (spectrum * norm_factor).reshape(1, own_pairs, window, 2, DEPTH)
-    all_stats = lax.dynamic_update_slice_in_dim(
-        jnp.zeros((stations, window, 8), jnp.float32),
-        baseline_stats,
-        tm_index * block_pairs,
-        0,
-    )
-    all_stats = lax.psum(all_stats.reshape(-1, 128), ("chan", "tm")).reshape(all_stats.shape) / CHANNELS
+    all_stats = lax.all_gather(
+        lax.psum(baseline_stats, "chan"), "tm", axis=0, tiled=True
+    ) / CHANNELS
     station_axis = jnp.arange(stations, dtype=jnp.int32)
     window_map = (window_stations[:, None] == station_axis[None, :]).astype(jnp.float32)
     station_map = jnp.eye(stations, dtype=jnp.float32)

time: 328 us -> 287 us (0.88)
  blocking collectives: 64.9 us -> 36.5 us
  local copies, waits for them, and re-layouts: 62.1 us -> 55.8 us
  other arithmetic: 66.6 us -> 60.5 us
    psum x1, blocking collectives: 64.9 us -> 13.4 us  [per_device(): lax.psum(baseline_stats, 'chan')]
    all_gather x0 -> x1, blocking collectives: none -> 23.1 us  [per_device(): lax.all_gather(lax.psum(baseline_stats, 'chan'), 'tm', axis=0, tiled=True)]
    slice x6 -> x0, local copies, waits for them, and re-layouts: 5.46 us -> none  [per_device(): fields = [all_stats[:, :, column] for column in range(8)]]
    reduce_sum x1, other arithmetic: 4.53 us -> 0.12 us  [station_terms(): jnp.sum(fields[7], 1)[:, None]]
  transfers between devices with their start and end apart: 2 -> 2, of which waited for: 2 -> 2; matrix products, arithmetic and copies ran while one was open for 10% -> 12% of each run, Pallas kernels for 0% -> 0%
where the time goes in v3:
time: 287 us; the launch traced here: 286 us
  waiting for transfers between devices  82.6 us (29%)
  other arithmetic  60.5 us (21%)
  local copies, waits for them, and re-layouts  55.8 us (19%)
  blocking collectives  36.5 us (13%)
  matrix products  35.7 us (12%)
  between operations  14.3 us (5%)
    reduce_scatter x1, waiting for transfers between devices, per_device(): lax.psum_scatter(partial.reshape(partial_shape[0], -1, partial_shape[-1])...  56.2 us
    unnamed x10, local copies, waits for them, and re-layouts  29.7 us
    reduce_scatter x1, waiting for transfers between devices, per_device(): lax.psum_scatter(spectrum.reshape(block_pairs // 2, -1, DEPTH), 'chan', s...  26.4 us
    dot_general x1, matrix products, per_device(): jnp.einsum('tcaw,tcbx->xbawc', picked, voltages, preferred_element_type=j...  23.3 us
    all_gather x1, blocking collectives, per_device(): lax.all_gather(lax.psum(baseline_stats, 'chan'), 'tm', axis=0, tiled=True)  23.1 us
    convert_element_type x1, other arithmetic, phase_table(): jnp.sin(angles).astype(jnp.bfloat16)  17 us
    neg x1, other arithmetic, add_block(): -sine_part  14.4 us
    another operation x1, local copies, waits for them, and re-layouts, per_device(): jnp.stack([blocks[:, 0, 0] + blocks[:, 1, 1], blocks[:, 0, 1] - blocks[:,...  13.7 us
  transfers between devices with their start and end apart: 2, of which 2 were waited for; matrix products, arithmetic and copies ran while one was open for 12% of the time, Pallas kernels for 0%

profile of v3, /device:TPU:0, one launch (start us, length us, event | category | flops | bytes accessed | tf_op | source)
XLA Modules:
  0.0 285.7 jit_solution(16615988717630603320)
XLA Ops:
  7.2 0.7 broadcast_multiply_fusion.3
  8.1 29.7 %copy.84 = bf16[8,1024,2,512]{1,0,2,3:T(8,128)(2,1)} copy(bf16[8,1024,2,512]{3,2,1,0:T(2,128)(2,1)} %param.3) | data formatting | bytes 33554432 | tf_op args[0]
  37.8 6.3 %gather_fusion = bf16[4,8,1024,2]{2,1,3,0:T(8,128)(2,1)S(1)} fusion(bf16[8,1024,2,512]{1,0,2,3:T(8,128)(2,1)} %copy.84, s32[1024]{0:T(1024)S(1)} %pad_clamp_fusion), kind=kCustom, calls=%fused_computation | custom fusion | bytes 262160 | tf_op jit(solution)/shard_map/jit(_take)/gather | solution.py:118
  44.2 1.4 copy.104
  45.6 23.3 %fusion.2 = f32[512,2,2,4,1024]{0,3,1,2,4:T(4,128)} fusion(bf16[8,1024,2,4,1]{0,3,4,2,1:T(4,128)(2,1)S(1)} %copy.104, bf16[8,1024,2,512,1]{3,2,1,0,4:T(2,128)(2,1)} %bitcast.189), kind=kOutput, calls=%fused_computation.3 | convolution fusion | flops 134217728 | bytes 50462720 | tf_op jit(solution)/shard_map/tcaw,tcbx->xbawc/dot_general | solution.py:119
  68.9 7.1 %fusion.18 = bf16[512,1,4,1024]{0,2,3,1:T(4,128)(2,1)S(1)} fusion(f32[512,2,2,4,1024]{0,3,1,2,4:T(4,128)} %fusion.2), kind=kLoop, calls=%fused_computation.23 | loop fusion | flops 4194304 | bytes 20971520 | tf_op jit(solution)/shard_map/add | solution.py:121
  76.0 7.1 %fusion.19 = bf16[512,1,4,1024]{0,2,3,1:T(4,128)(2,1)S(1)} fusion(f32[512,2,2,4,1024]{0,3,1,2,4:T(4,128)} %fusion.2), kind=kLoop, calls=%fused_computation.24 | loop fusion | flops 4194304 | bytes 20971520 | tf_op jit(solution)/shard_map/sub | solution.py:121
  83.1 7.4 %pad_maximum_fusion = bf16[512,2,4,1024]{0,2,3,1:T(4,128)(2,1)} fusion(bf16[512,1,4,1024]{0,2,3,1:T(4,128)(2,1)S(1)} %fusion.19, bf16[512,1,4,1024]{0,2,3,1:T(4,128)(2,1)S(1)} %fusion.18), kind=kLoop, calls=%fused_computation.10 | loop fusion | flops 4194304 | bytes 16777216 | tf_op jit(solution)/shard_map/stack | solution.py:120
  90.5 13.7 %copy.89 = bf16[512,2,4,1024]{3,0,2,1:T(8,128)(2,1)} copy(bf16[512,2,4,1024]{0,2,3,1:T(4,128)(2,1)} %pad_maximum_fusion) | data formatting | bytes 16777216 | tf_op jit(solution)/shard_map/stack | solution.py:120
  104.5 0.7 broadcast_multiply_fusion.2
  105.2 14.4 %fusion.20 = bf16[1024,1024]{1,0:T(8,128)(2,1)S(1)} fusion(f32[1024]{0:T(1024)S(1)} %get-tuple-element.80, f32[1024]{0:T(1024)S(1)} %get-tuple-element.81), kind=kLoop, calls=%fused_computation.25 | loop fusion | flops 5242880 | bytes 2105344 | tf_op jit(solution)/shard_map/while/body/eval_jaxpr/neg | solution.py:95
  119.6 17.0 %fusion.17 = (bf16[1024,1024]{1,0:T(8,128)(2,1)}, bf16[1024,1024]{1,0:T(8,128)(2,1)}) fusion(f32[1024]{0:T(1024)S(1)} %get-tuple-element.80, f32[1024]{0:T(1024)S(1)} %get-tuple-element.81), kind=kLoop, calls=%fused_computation.22 | loop fusion | flops 3145728 | bytes 4202496 | tf_op jit(solution)/shard_map/while/body/eval_jaxpr/convert_element_type | solution.py:19
  136.7 56.2 %reduce-scatter.3.cloned.1.call-done = bf16[32,8,1024]{2,0,1:T(8,128)(2,1)} async-done(((bf16[512,8,1024]{2,0,1:T(8,128)(2,1)}), bf16[32,8,1024]{2,0,1:T(8,128)(2,1)}) %reduce-scatter.3.cloned.1.call-update) | async-done | bytes 524304 | tf_op jit(solution)/shard_map/reduce_scatter | solution.py:124
  192.9 1.2 reshape_reshape.6
  194.1 0.9 fusion.41
  195.8 1.0 fusion.33
  197.5 13.4 %psum.7 = f32[16,2,8]{0,1,2:T(2,128)S(1)} all-reduce(f32[16,2,8]{0,1,2:T(2,128)S(1)} %constant_dynamic-update-slice_fusion), channel_id=1, replica_groups=mesh['chan'=8,'tm'=16] {'chan'}, use_global_device_ids=true, to_apply=%region_10.11 | all-reduce | flops 256 | bytes 2048 | tf_op jit(solution)/shard_map/psum | solution.py:146
  211.0 23.1 %all_gather.3 = f32[256,2,8]{2,1,0:T(2,128)S(1)} all-gather(f32[16,2,8]{2,1,0:T(2,128)S(1)} %copy.102), channel_id=1, replica_groups=mesh['chan'=8,'tm'=16] {'tm'}, dimensions={0}, use_global_device_ids=true | all-gather | bytes 17408 | tf_op jit(solution)/shard_map/all_gather | solution.py:145
  237.1 12.4 %fusion.8 = f32[32,2048]{1,0:T(8,128)S(1)} fusion(bf16[1024,1024]{1,0:T(8,128)(2,1)} %get-tuple-element.75, bf16[1024,1024]{1,0:T(8,128)(2,1)} %get-tuple-element.74, bf16[1024,1024]{1,0:T(8,128)(2,1)S(1)} %fusion.20, bf16[32,1024]{1,0:T(8,128)(2,1)S(1)} %multiply_convert_fusion, bf16[32,1024]{1,0:T(8,128)(2,1)S(1)} %multiply_convert_fusion.1), kind=kOutput, calls=%fused_computation.11 | convolution fusion | flops 302252032 | bytes 6684672 | tf_op jit(solution)/shard_map/while/body/eval_jaxpr/dot_general | solution.py:97
  249.5 0.7 reshape_reshape.7
  250.5 0.6 pad_maximum_fusion.1
  251.1 26.4 %reduce-scatter.5.cloned.1.call-done = f32[1,8,1024]{2,1,0:T(8,128)} async-done(((f32[8,8,1024]{2,1,0:T(8,128)}), f32[1,8,1024]{2,1,0:T(8,128)}) %reduce-scatter.5.cloned.1.call-update) | async-done | bytes 32784 | tf_op jit(solution)/shard_map/reduce_scatter | solution.py:140
  277.4 0.8 broadcast_multiply_fusion
  278.2 0.6 reshape.289
  (67 shorter events, 5.4 us)
Async XLA Ops:
  7.2 185.7 %reduce-scatter.3.cloned.1.call-start = ((), (), s32[]{:S(2)}) async-start(), calls=%async_computation.2 | async-start | bytes 8912896 | tf_op jit(solution)/shard_map/reduce_scatter | solution.py:124
  104.3 130.5 %copy-start = (s32[2]{0:T(128)S(1)}, s32[2]{0:T(128)}, u32[]{:S(2)}) copy-start(s32[2]{0:T(128)} %param.4) | copy-start | bytes 28
  104.3 173.1 %reduce-scatter.5.cloned.1.call-start = ((), (), s32[]{:S(2)}) async-start(), calls=%async_computation.3 | async-start | bytes 294912 | tf_op jit(solution)/shard_map/reduce_scatter | solution.py:140
Sparse Core Ops, SparseCore 0:
  104.4 88.4 reduce-scatter.2
  250.4 27.0 reduce-scatter.4

commit v4 on v3

--- a/solution.py
+++ b/solution.py
@@ -115,14 +115,23 @@
     feed_index = (2 * window_stations[:, None] + jnp.arange(2, dtype=jnp.int32)[None, :]).reshape(
         -1
     )
-    picked = jnp.take(voltages, feed_index, axis=3)
-    blocks = jnp.einsum("tcaw,tcbx->xbawc", picked, voltages, preferred_element_type=jnp.float32)
-    partial = jnp.stack(
-        [blocks[:, 0, 0] + blocks[:, 1, 1], blocks[:, 0, 1] - blocks[:, 1, 0]], 1
+    picked = jnp.concatenate(
+        [
+            lax.dynamic_slice_in_dim(voltages, 2 * window_stations[k], 2, 3)
+            for k in range(window)
+        ],
+        3,
+    )
+    left = jnp.stack(
+        [picked, jnp.stack([picked[:, :, 1], -picked[:, :, 0]], 2)], 3
+    )
+    left = left.reshape(*picked.shape[:3], -1)
+    partial = jnp.einsum(
+        "tcrq,tcri->iqc", left, voltages, preferred_element_type=jnp.float32
     ).astype(jnp.bfloat16)
-    partial_shape = partial.shape
+    partial_shape = (inputs, 2, 2 * window, channel_count)
     summed = lax.psum_scatter(
-        partial.reshape(partial_shape[0], -1, partial_shape[-1]),
+        partial,
         "tm",
         scatter_dimension=0,
         tiled=True,

time: 287 us -> 253 us (0.88)
  other arithmetic: 60.5 us -> 37.1 us
  local copies, waits for them, and re-layouts: 55.8 us -> 48.7 us
  matrix products: 35.7 us -> 31.6 us
    unnamed x10 -> x11, local copies, waits for them, and re-layouts: 29.7 us -> 12.3 us
    convert_element_type x0 -> x1, local copies, waits for them, and re-layouts: none -> 13.6 us  [per_device(): partial = jnp.einsum('tcrq,tcri->iqc', left, voltages, preferred_element_...]
    dynamic_slice x0 -> x1, local copies, waits for them, and re-layouts: none -> 11.9 us  [per_device(): lax.dynamic_slice_in_dim(voltages, 2 * window_stations[k], 2, 3)]
    another operation x1, local copies, waits for them, and re-layouts: 13.7 us -> 5.26 us  [per_device(): jnp.stack([picked, jnp.stack([picked[:, :, 1], -picked[:, :, 0]], 2)], 3)]
    another operation x1 -> x2, other arithmetic: 7.39 us -> 0.06 us  [per_device(): jnp.stack([picked, jnp.stack([picked[:, :, 1], -picked[:, :, 0]], 2)], 3)]
    add x2 -> x0, other arithmetic: 7.17 us -> none  [the longest x1 7.1 us: per_device(): blocks[:, 0, 0] + blocks[:, 1, 1]]
    sub x1 -> x0, other arithmetic: 7.11 us -> none  [per_device(): blocks[:, 0, 1] - blocks[:, 1, 0]]
    gather x1 -> x0, local copies, waits for them, and re-layouts: 6.32 us -> none  [per_device(): picked = jnp.take(voltages, feed_index, axis=3)]
  transfers between devices with their start and end apart: 2 -> 2, of which waited for: 2 -> 2; matrix products, arithmetic and copies ran while one was open for 12% -> 13% of each run, Pallas kernels for 0% -> 0%
where the time goes in v4:
time: 253 us; the launch traced here: 252 us
  waiting for transfers between devices  82.8 us (33%)
  local copies, waits for them, and re-layouts  48.7 us (19%)
  other arithmetic  37.1 us (15%)
  blocking collectives  36.5 us (14%)
  matrix products  31.6 us (12%)
  between operations  15.6 us (6%)
    reduce_scatter x1, waiting for transfers between devices, per_device(): lax.psum_scatter(partial, 'tm', scatter_dimension=0, tiled=True)  56.4 us
    reduce_scatter x1, waiting for transfers between devices, per_device(): lax.psum_scatter(spectrum.reshape(block_pairs // 2, -1, DEPTH), 'chan', s...  26.4 us
    all_gather x1, blocking collectives, per_device(): lax.all_gather(lax.psum(baseline_stats, 'chan'), 'tm', axis=0, tiled=True)  23.1 us
    dot_general x1, matrix products, per_device(): jnp.einsum('tcrq,tcri->iqc', left, voltages, preferred_element_type=jnp.f...  19.2 us
    convert_element_type x1, other arithmetic, phase_table(): jnp.sin(angles).astype(jnp.bfloat16)  17 us
    neg x1, other arithmetic, add_block(): -sine_part  14.4 us
    convert_element_type x1, local copies, waits for them, and re-layouts, per_device(): partial = jnp.einsum('tcrq,tcri->iqc', left, voltages, preferred_element_...  13.6 us
    psum x1, blocking collectives, per_device(): lax.psum(baseline_stats, 'chan')  13.4 us
  transfers between devices with their start and end apart: 2, of which 2 were waited for; matrix products, arithmetic and copies ran while one was open for 13% of the time, Pallas kernels for 0%

profile of v4, /device:TPU:0, one launch (start us, length us, event | category | flops | bytes accessed | tf_op | source)
XLA Modules:
  0.0 252.5 jit_solution(10175118800439471353)
XLA Ops:
  7.2 1.3 fusion.40
  9.8 11.9 %constant_dynamic-slice_fusion = (bf16[8,1024,2,2]{3,2,1,0:T(2,128)(2,1)}, bf16[8,1024,2,2]{3,2,1,0:T(2,128)(2,1)}) fusion(bf16[8,1024,2,512]{3,2,1,0:T(2,128)(2,1)} %param.3, s32[]{:T(128)S(6)} %select_n.13, s32[]{:T(128)S(6)} %select_n.12), kind=kLoop, calls=%fused_computation.129 | loop fusion | bytes 262152 | tf_op jit(solution)/shard_map/dynamic_slice | solution.py:120
  21.7 6.1 %copy.161 = bf16[8,1024,2,2]{1,0,3,2:T(8,128)(2,1)S(1)} copy(bf16[8,1024,2,2]{3,2,1,0:T(2,128)(2,1)} %get-tuple-element.64) | data formatting | bytes 131072
  27.8 6.1 %copy.162 = bf16[8,1024,2,2]{1,0,3,2:T(8,128)(2,1)S(1)} copy(bf16[8,1024,2,2]{3,2,1,0:T(2,128)(2,1)} %get-tuple-element.63) | data formatting | bytes 131072
  34.1 5.3 %copy.125 = bf16[8,1024,2,2,4]{0,4,3,2,1:T(4,128)(2,1)} copy(bf16[8,1024,2,2,4]{1,0,4,2,3:T(8,128)(2,1)S(1)} %pad_maximum_fusion) | data formatting | bytes 524288 | tf_op jit(solution)/shard_map/stack | solution.py:125
  39.3 19.2 %fusion.2 = bf16[512,8,1024]{0,1,2:T(8,128)(2,1)} fusion(bf16[8,1024,2,8]{0,3,2,1:T(8,128)(2,1)} %bitcast.173, bf16[8,1024,2,512]{3,2,1,0:T(2,128)(2,1)} %param.3), kind=kOutput, calls=%fused_computation.3 | convolution fusion | flops 138412032 | bytes 25427968 | tf_op jit(solution)/shard_map/tcrq,tcri->iqc/dot_general | solution.py:129
  58.5 13.6 %copy.127 = bf16[512,8,1024]{2,1,0:T(8,128)(2,1)} copy(bf16[512,8,1024]{0,1,2:T(8,128)(2,1)} %fusion.2) | data formatting | bytes 16777216 | tf_op jit(solution)/shard_map/convert_element_type | solution.py:131
  72.1 0.2 reduce-scatter.5.cloned.1.call-start
  72.4 0.7 broadcast_multiply_fusion.2
  73.1 14.4 %fusion.15 = bf16[1024,1024]{1,0:T(8,128)(2,1)S(1)} fusion(f32[1024]{0:T(1024)S(1)} %get-tuple-element.86, f32[1024]{0:T(1024)S(1)} %get-tuple-element.87), kind=kLoop, calls=%fused_computation.16 | loop fusion | flops 5242880 | bytes 2105344 | tf_op jit(solution)/shard_map/while/body/eval_jaxpr/neg | solution.py:95
  87.5 17.0 %fusion.14 = (bf16[1024,1024]{1,0:T(8,128)(2,1)}, bf16[1024,1024]{1,0:T(8,128)(2,1)}) fusion(f32[1024]{0:T(1024)S(1)} %get-tuple-element.86, f32[1024]{0:T(1024)S(1)} %get-tuple-element.87), kind=kLoop, calls=%fused_computation.15 | loop fusion | flops 3145728 | bytes 4202496 | tf_op jit(solution)/shard_map/while/body/eval_jaxpr/convert_element_type | solution.py:19
  104.5 56.4 %reduce-scatter.3.cloned.1.call-done = bf16[32,8,1024]{2,1,0:T(8,128)(2,1)} async-done(((bf16[512,8,1024]{2,1,0:T(8,128)(2,1)}), bf16[32,8,1024]{2,1,0:T(8,128)(2,1)}) %reduce-scatter.3.cloned.1.call-update) | async-done | bytes 524304 | tf_op jit(solution)/shard_map/reduce_scatter | solution.py:133
  160.9 1.2 reshape_reshape.6
  162.1 1.1 fusion.39
  163.8 0.3 fusion.29
  164.1 13.4 %psum.7 = f32[16,2,8]{0,1,2:T(2,128)S(1)} all-reduce(f32[16,2,8]{0,1,2:T(2,128)S(1)} %constant_dynamic-update-slice_fusion), channel_id=1, replica_groups=mesh['chan'=8,'tm'=16] {'chan'}, use_global_device_ids=true, to_apply=%region_10.0 | all-reduce | flops 256 | bytes 2048 | tf_op jit(solution)/shard_map/psum | solution.py:155
  177.6 23.1 %all_gather.3 = f32[256,2,8]{2,1,0:T(2,128)S(1)} all-gather(f32[16,2,8]{2,1,0:T(2,128)S(1)} %copy.150), channel_id=1, replica_groups=mesh['chan'=8,'tm'=16] {'tm'}, dimensions={0}, use_global_device_ids=true | all-gather | bytes 17408 | tf_op jit(solution)/shard_map/all_gather | solution.py:154
  201.7 0.2 select_reduce_fusion.17
  203.9 12.4 %fusion.3 = f32[32,2048]{1,0:T(8,128)S(1)} fusion(bf16[1024,1024]{1,0:T(8,128)(2,1)} %get-tuple-element.79, bf16[1024,1024]{1,0:T(8,128)(2,1)} %get-tuple-element.78, bf16[1024,1024]{1,0:T(8,128)(2,1)S(1)} %fusion.15, bf16[32,1024]{1,0:T(8,128)(2,1)S(1)} %multiply_convert_fusion, bf16[32,1024]{1,0:T(8,128)(2,1)S(1)} %multiply_convert_fusion.1), kind=kOutput, calls=%fused_computation.4 | convolution fusion | flops 302252032 | bytes 6684672 | tf_op jit(solution)/shard_map/while/body/eval_jaxpr/dot_general | solution.py:97
  216.3 0.7 reshape_reshape.7
  217.3 0.6 pad_maximum_fusion.2
  217.8 26.4 %reduce-scatter.5.cloned.1.call-done = f32[1,8,1024]{2,1,0:T(8,128)} async-done(((f32[8,8,1024]{2,1,0:T(8,128)}), f32[1,8,1024]{2,1,0:T(8,128)}) %reduce-scatter.5.cloned.1.call-update) | async-done | bytes 32784 | tf_op jit(solution)/shard_map/reduce_scatter | solution.py:149
  244.2 0.8 broadcast_multiply_fusion
  245.0 0.6 reshape.215
  (57 shorter events, 3.9 us)
Async XLA Ops:
  7.2 153.7 %reduce-scatter.3.cloned.1.call-start = ((), (), s32[]{:S(2)}) async-start(), calls=%async_computation.2 | async-start | bytes 8912896 | tf_op jit(solution)/shard_map/reduce_scatter | solution.py:133
  72.1 172.1 %reduce-scatter.5.cloned.1.call-start = ((), (), s32[]{:S(2)}) async-start(), calls=%async_computation.3 | async-start | bytes 294912 | tf_op jit(solution)/shard_map/reduce_scatter | solution.py:149
  87.5 114.0 %copy-start = (s32[2]{0:T(128)S(1)}, s32[2]{0:T(128)}, u32[]{:S(2)}) copy-start(s32[2]{0:T(128)} %param.4) | copy-start | bytes 28
Sparse Core Ops, SparseCore 0:
  72.3 88.5 reduce-scatter.2
  217.2 27.0 reduce-scatter.4

commit v5 on v4

--- a/solution.py
+++ b/solution.py
@@ -115,13 +115,12 @@
     feed_index = (2 * window_stations[:, None] + jnp.arange(2, dtype=jnp.int32)[None, :]).reshape(
         -1
     )
-    picked = jnp.concatenate(
-        [
-            lax.dynamic_slice_in_dim(voltages, 2 * window_stations[k], 2, 3)
-            for k in range(window)
-        ],
-        3,
-    )
+    selector = (
+        jnp.arange(inputs, dtype=jnp.int32)[:, None] == feed_index[None, :]
+    ).astype(voltages.dtype)
+    picked = jnp.einsum(
+        "tcri,iw->tcrw", voltages, selector, preferred_element_type=jnp.float32
+    ).astype(voltages.dtype)
     left = jnp.stack(
         [picked, jnp.stack([picked[:, :, 1], -picked[:, :, 0]], 2)], 3
     )

time: 253 us -> 237 us (0.937)
  local copies, waits for them, and re-layouts: 48.7 us -> 22.9 us
  matrix products: 31.6 us -> 42 us
    unnamed x11 -> x9, local copies, waits for them, and re-layouts: 12.3 us -> 0.06 us
    dynamic_slice x1 -> x0, local copies, waits for them, and re-layouts: 11.9 us -> none  [per_device(): lax.dynamic_slice_in_dim(voltages, 2 * window_stations[k], 2, 3)]
    dot_general x0 -> x1, matrix products: none -> 10.4 us  [per_device(): jnp.einsum('tcri,iw->tcrw', voltages, selector, preferred_element_type=jn...]
    another operation x1, local copies, waits for them, and re-layouts: 5.26 us -> 0.15 us  [per_device(): jnp.stack([picked, jnp.stack([picked[:, :, 1], -picked[:, :, 0]], 2)], 3)]
    reshape x0 -> x1, local copies, waits for them, and re-layouts: none -> 4.72 us  [per_device(): left = left.reshape(*picked.shape[:3], -1)]
  transfers between devices with their start and end apart: 2 -> 2, of which waited for: 2 -> 2; matrix products, arithmetic and copies ran while one was open for 13% -> 14% of each run, Pallas kernels for 0% -> 0%
where the time goes in v5:
time: 237 us
  waiting for transfers between devices  82.9 us (35%)
  matrix products  42 us (18%)
  other arithmetic  38.1 us (16%)
  blocking collectives  36.5 us (15%)
  local copies, waits for them, and re-layouts  22.9 us (10%)
  between operations  14.3 us (6%)
    reduce_scatter x1, waiting for transfers between devices, per_device(): lax.psum_scatter(partial, 'tm', scatter_dimension=0, tiled=True)  56.4 us
    reduce_scatter x1, waiting for transfers between devices, per_device(): lax.psum_scatter(spectrum.reshape(block_pairs // 2, -1, DEPTH), 'chan', s...  26.4 us
    all_gather x1, blocking collectives, per_device(): lax.all_gather(lax.psum(baseline_stats, 'chan'), 'tm', axis=0, tiled=True)  23.1 us
    dot_general x1, matrix products, per_device(): jnp.einsum('tcrq,tcri->iqc', left, voltages, preferred_element_type=jnp.f...  19.2 us
    convert_element_type x1, other arithmetic, phase_table(): jnp.sin(angles).astype(jnp.bfloat16)  17 us
    neg x1, other arithmetic, add_block(): -sine_part  14.4 us
    convert_element_type x1, local copies, waits for them, and re-layouts, per_device(): partial = jnp.einsum('tcrq,tcri->iqc', left, voltages, preferred_element_...  13.6 us
    psum x1, blocking collectives, per_device(): lax.psum(baseline_stats, 'chan')  13.4 us
  transfers between devices with their start and end apart: 2, of which 2 were waited for; matrix products, arithmetic and copies ran while one was open for 14% of the time, Pallas kernels for 0%

profile of v5, /device:TPU:0, one launch (start us, length us, event | category | flops | bytes accessed | tf_op | source)
XLA Modules:
  0.0 236.8 jit_solution(7555849971387422699)
XLA Ops:
  7.2 0.7 broadcast_multiply_fusion.3
  8.0 10.4 %fusion.17 = bf16[4,8,1024,2]{2,0,3,1:T(4,128)(2,1)S(1)} fusion(bf16[8,1024,2,512]{3,2,1,0:T(2,128)(2,1)} %param.3, s32[4]{0:T(128)S(1)} %add.255), kind=kOutput, calls=%fused_computation.18 | convolution fusion | flops 67176448 | bytes 16908304 | tf_op jit(solution)/shard_map/tcri,iw->tcrw/dot_general | solution.py:121
  18.6 0.2 pad_maximum_fusion
  19.0 4.7 %copy.123 = bf16[8,1024,2,8]{0,3,2,1:T(8,128)(2,1)} copy(bf16[8,1024,2,8]{1,0,3,2:T(8,128)(2,1)S(1)} %bitcast.179) | data formatting | bytes 524288 | tf_op jit(solution)/shard_map/reshape | solution.py:127
  23.7 19.2 %fusion.4 = bf16[512,8,1024]{0,1,2:T(8,128)(2,1)} fusion(bf16[8,1024,2,8]{0,3,2,1:T(8,128)(2,1)} %copy.123, bf16[8,1024,2,512]{3,2,1,0:T(2,128)(2,1)} %param.3), kind=kOutput, calls=%fused_computation.5 | convolution fusion | flops 138412032 | bytes 25427968 | tf_op jit(solution)/shard_map/tcrq,tcri->iqc/dot_general | solution.py:128
  42.9 13.6 %copy.125 = bf16[512,8,1024]{2,1,0:T(8,128)(2,1)} copy(bf16[512,8,1024]{0,1,2:T(8,128)(2,1)} %fusion.4) | data formatting | bytes 16777216 | tf_op jit(solution)/shard_map/convert_element_type | solution.py:130
  56.6 0.7 broadcast_multiply_fusion.2
  57.3 14.4 %fusion.20 = bf16[1024,1024]{1,0:T(8,128)(2,1)S(1)} fusion(f32[1024]{0:T(1024)S(1)} %get-tuple-element.82, f32[1024]{0:T(1024)S(1)} %get-tuple-element.83), kind=kLoop, calls=%fused_computation.19 | loop fusion | flops 5242880 | bytes 2105344 | tf_op jit(solution)/shard_map/while/body/eval_jaxpr/neg | solution.py:95
  71.7 17.0 %fusion.16 = (bf16[1024,1024]{1,0:T(8,128)(2,1)}, bf16[1024,1024]{1,0:T(8,128)(2,1)}) fusion(f32[1024]{0:T(1024)S(1)} %get-tuple-element.82, f32[1024]{0:T(1024)S(1)} %get-tuple-element.83), kind=kLoop, calls=%fused_computation.17 | loop fusion | flops 3145728 | bytes 4202496 | tf_op jit(solution)/shard_map/while/body/eval_jaxpr/convert_element_type | solution.py:19
  88.7 56.4 %reduce-scatter.3.cloned.1.call-done = bf16[32,8,1024]{2,1,0:T(8,128)(2,1)} async-done(((bf16[512,8,1024]{2,1,0:T(8,128)(2,1)}), bf16[32,8,1024]{2,1,0:T(8,128)(2,1)}) %reduce-scatter.3.cloned.1.call-update) | async-done | bytes 524304 | tf_op jit(solution)/shard_map/reduce_scatter | solution.py:132
  145.1 1.2 reshape_reshape.6
  146.4 1.1 fusion.43
  147.7 0.3 fusion.28
  148.0 0.3 fusion.33
  148.4 13.4 %psum.7 = f32[16,2,8]{0,1,2:T(2,128)S(1)} all-reduce(f32[16,2,8]{0,1,2:T(2,128)S(1)} %constant_dynamic-update-slice_fusion), channel_id=1, replica_groups=mesh['chan'=8,'tm'=16] {'chan'}, use_global_device_ids=true, to_apply=%region_10.0 | all-reduce | flops 256 | bytes 2048 | tf_op jit(solution)/shard_map/psum | solution.py:154
  161.9 23.1 %all_gather.3 = f32[256,2,8]{2,1,0:T(2,128)S(1)} all-gather(f32[16,2,8]{2,1,0:T(2,128)S(1)} %copy.148), channel_id=1, replica_groups=mesh['chan'=8,'tm'=16] {'tm'}, dimensions={0}, use_global_device_ids=true | all-gather | bytes 17408 | tf_op jit(solution)/shard_map/all_gather | solution.py:153
  186.0 0.2 select_reduce_fusion.17
  186.9 0.2 select_reduce_fusion.13
  188.2 12.4 %fusion.5 = f32[32,2048]{1,0:T(8,128)S(1)} fusion(bf16[1024,1024]{1,0:T(8,128)(2,1)} %get-tuple-element.77, bf16[1024,1024]{1,0:T(8,128)(2,1)} %get-tuple-element.76, bf16[1024,1024]{1,0:T(8,128)(2,1)S(1)} %fusion.20, bf16[32,1024]{1,0:T(8,128)(2,1)S(1)} %multiply_convert_fusion, bf16[32,1024]{1,0:T(8,128)(2,1)S(1)} %multiply_convert_fusion.1), kind=kOutput, calls=%fused_computation.6 | convolution fusion | flops 302252032 | bytes 6684672 | tf_op jit(solution)/shard_map/while/body/eval_jaxpr/dot_general | solution.py:97
  200.6 0.7 reshape_reshape.7
  201.5 0.6 pad_maximum_fusion.1
  202.1 26.4 %reduce-scatter.5.cloned.1.call-done = f32[1,8,1024]{2,1,0:T(8,128)} async-done(((f32[8,8,1024]{2,1,0:T(8,128)}), f32[1,8,1024]{2,1,0:T(8,128)}) %reduce-scatter.5.cloned.1.call-update) | async-done | bytes 32784 | tf_op jit(solution)/shard_map/reduce_scatter | solution.py:148
  228.6 0.8 broadcast_multiply_fusion
  229.3 0.6 reshape.227
  (57 shorter events, 3.8 us)
Async XLA Ops:
  7.2 138.0 %reduce-scatter.3.cloned.1.call-start = ((), (), s32[]{:S(2)}) async-start(), calls=%async_computation.2 | async-start | bytes 8912896 | tf_op jit(solution)/shard_map/reduce_scatter | solution.py:132
  56.5 172.0 %reduce-scatter.5.cloned.1.call-start = ((), (), s32[]{:S(2)}) async-start(), calls=%async_computation.3 | async-start | bytes 294912 | tf_op jit(solution)/shard_map/reduce_scatter | solution.py:148
  71.7 114.0 %copy-start = (s32[2]{0:T(128)S(1)}, s32[2]{0:T(128)}, u32[]{:S(2)}) copy-start(s32[2]{0:T(128)} %param.4) | copy-start | bytes 28
Sparse Core Ops, SparseCore 0:
  56.6 88.4 reduce-scatter.2
  201.4 27.0 reduce-scatter.4

commit v6 on v3

--- a/solution.py
+++ b/solution.py
@@ -8,6 +8,7 @@
 CHANNELS = 8192
 DEPTH = 1024
 ITERATIONS = 3
+TM_CHUNKS = 2
 
 
 def phase_table(first_channel, channel_count):
@@ -115,18 +116,25 @@
     feed_index = (2 * window_stations[:, None] + jnp.arange(2, dtype=jnp.int32)[None, :]).reshape(
         -1
     )
-    picked = jnp.take(voltages, feed_index, axis=3)
-    blocks = jnp.einsum("tcaw,tcbx->xbawc", picked, voltages, preferred_element_type=jnp.float32)
-    partial = jnp.stack(
-        [blocks[:, 0, 0] + blocks[:, 1, 1], blocks[:, 0, 1] - blocks[:, 1, 0]], 1
-    ).astype(jnp.bfloat16)
-    partial_shape = partial.shape
-    summed = lax.psum_scatter(
-        partial.reshape(partial_shape[0], -1, partial_shape[-1]),
-        "tm",
-        scatter_dimension=0,
-        tiled=True,
-    ).reshape(-1, *partial_shape[1:])
+    selector = (
+        jnp.arange(inputs, dtype=jnp.int32)[:, None] == feed_index[None, :]
+    ).astype(voltages.dtype)
+    chunk = channel_count // TM_CHUNKS
+    pieces = []
+    for part in range(TM_CHUNKS):
+        block = voltages[:, part * chunk : (part + 1) * chunk]
+        picked = jnp.einsum(
+            "tcri,iw->tcrw", block, selector, preferred_element_type=jnp.float32
+        ).astype(voltages.dtype)
+        left = jnp.stack(
+            [picked, jnp.stack([picked[:, :, 1], -picked[:, :, 0]], 2)], 3
+        )
+        left = left.reshape(*picked.shape[:3], -1)
+        partial = jnp.einsum(
+            "tcrq,tcri->iqc", left, block, preferred_element_type=jnp.float32
+        ).astype(jnp.bfloat16)
+        pieces.append(lax.psum_scatter(partial, "tm", scatter_dimension=0, tiled=True))
+    summed = jnp.concatenate(pieces, 2).reshape(-1, 2, 2 * window, channel_count)
     chan_index = lax.axis_index("chan")
     tm_index = lax.axis_index("tm")
     first_channel = chan_index * channel_count

time: 287 us -> 302 us (1.052)
  waiting for transfers between devices: 82.6 us -> 130 us
  other arithmetic: 60.5 us -> 38.5 us
  local copies, waits for them, and re-layouts: 55.8 us -> 39 us
  matrix products: 35.7 us -> 44.1 us
    reduce_scatter x1 -> x2, waiting for transfers between devices: 56.2 us -> 103 us  [per_device(): lax.psum_scatter(partial, 'tm', scatter_dimension=0, tiled=True)]
    unnamed x10 -> x9, local copies, waits for them, and re-layouts: 29.7 us -> 0.06 us
    convert_element_type x0 -> x2, local copies, waits for them, and re-layouts: none -> 17.3 us  [per_device(): partial = jnp.einsum('tcrq,tcri->iqc', left, block, preferred_element_typ...]
    slice x0 -> x1, local copies, waits for them, and re-layouts: none -> 14.2 us  [per_device(): block = voltages[:, part * chunk:(part + 1) * chunk]]
    another operation x1 -> x2, local copies, waits for them, and re-layouts: 13.7 us -> 0.09 us  [per_device(): jnp.stack([picked, jnp.stack([picked[:, :, 1], -picked[:, :, 0]], 2)], 3)]
    dot_general x1 -> x4, matrix products: 23.3 us -> 31.7 us  [the longest x2 20.4 us: per_device(): jnp.einsum('tcrq,tcri->iqc', left, block, preferred_element_type=jnp.floa...]
    another operation x1 -> x4, other arithmetic: 7.39 us -> 0.28 us  [per_device(): jnp.stack([picked, jnp.stack([picked[:, :, 1], -picked[:, :, 0]], 2)], 3)]
    sub x1 -> x0, other arithmetic: 7.11 us -> none  [per_device(): blocks[:, 0, 1] - blocks[:, 1, 0]]
  transfers between devices with their start and end apart: 2 -> 3, of which waited for: 2 -> 3; matrix products, arithmetic and copies ran while one was open for 12% -> 20% of each run, Pallas kernels for 0% -> 0%
where the time goes in v6:
time: 302 us
  waiting for transfers between devices  130 us (43%)
  matrix products  44.1 us (15%)
  local copies, waits for them, and re-layouts  39 us (13%)
  other arithmetic  38.5 us (13%)
  blocking collectives  35.7 us (12%)
  between operations  14.1 us (5%)
    reduce_scatter x2, waiting for transfers between devices, per_device(): lax.psum_scatter(partial, 'tm', scatter_dimension=0, tiled=True)  103 us
    reduce_scatter x1, waiting for transfers between devices, per_device(): lax.psum_scatter(spectrum.reshape(block_pairs // 2, -1, DEPTH), 'chan', s...  26.6 us
    all_gather x1, blocking collectives, per_device(): lax.all_gather(lax.psum(baseline_stats, 'chan'), 'tm', axis=0, tiled=True)  22.6 us
    dot_general x2, matrix products, per_device(): jnp.einsum('tcrq,tcri->iqc', left, block, preferred_element_type=jnp.floa...  20.4 us
    convert_element_type x2, local copies, waits for them, and re-layouts, per_device(): partial = jnp.einsum('tcrq,tcri->iqc', left, block, preferred_element_typ...  17.3 us
    convert_element_type x1, other arithmetic, phase_table(): jnp.sin(angles).astype(jnp.bfloat16)  17 us
    neg x1, other arithmetic, add_block(): -sine_part  14.4 us
    slice x1, local copies, waits for them, and re-layouts, per_device(): block = voltages[:, part * chunk:(part + 1) * chunk]  14.2 us
  transfers between devices with their start and end apart: 3, of which 3 were waited for; matrix products, arithmetic and copies ran while one was open for 20% of the time, Pallas kernels for 0%

profile of v6, /device:TPU:0, one launch (start us, length us, event | category | flops | bytes accessed | tf_op | source)
XLA Modules:
  0.0 301.6 jit_solution(11430466528843086392)
XLA Ops:
  7.2 14.2 %fusion.55 = (bf16[8,512,2,512]{3,2,1,0:T(2,128)(2,1)}, bf16[8,512,2,512]{3,2,1,0:T(2,128)(2,1)}) fusion(bf16[8,1024,2,512]{3,2,1,0:T(2,128)(2,1)} %param.3), kind=kLoop, calls=%fused_computation.142 | loop fusion | bytes 33554432 | tf_op jit(solution)/shard_map/slice | solution.py:125
  21.6 5.6 %fusion.24 = bf16[4,8,512,2]{2,0,3,1:T(4,128)(2,1)S(1)} fusion(bf16[8,512,2,512]{3,2,1,0:T(2,128)(2,1)} %get-tuple-element.63, s32[4]{0:T(128)S(1)} %add.257), kind=kOutput, calls=%fused_computation.24 | convolution fusion | flops 33589248 | bytes 8454160 | tf_op jit(solution)/shard_map/tcri,iw->tcrw/dot_general | solution.py:126
  27.5 2.0 copy.144
  29.5 10.2 %fusion.18 = bf16[512,8,512]{0,1,2:T(8,128)(2,1)} fusion(bf16[8,512,2,8]{0,3,2,1:T(8,128)(2,1)S(1)} %copy.144, bf16[8,512,2,512]{3,2,1,0:T(2,128)(2,1)} %get-tuple-element.63), kind=kOutput, calls=%fused_computation.22 | convolution fusion | flops 69206016 | bytes 12713984 | tf_op jit(solution)/shard_map/tcrq,tcri->iqc/dot_general | solution.py:133
  39.7 8.7 %copy.146 = bf16[512,8,512]{2,1,0:T(8,128)(2,1)} copy(bf16[512,8,512]{0,1,2:T(8,128)(2,1)} %fusion.18) | data formatting | bytes 8388608 | tf_op jit(solution)/shard_map/convert_element_type | solution.py:135
  48.6 5.6 %fusion.27 = bf16[4,8,512,2]{2,0,3,1:T(4,128)(2,1)S(1)} fusion(bf16[8,512,2,512]{3,2,1,0:T(2,128)(2,1)} %get-tuple-element.64, s32[4]{0:T(128)S(1)} %add.257), kind=kOutput, calls=%fused_computation.25 | convolution fusion | flops 33589248 | bytes 8454160 | tf_op jit(solution)/shard_map/tcri,iw->tcrw/dot_general | solution.py:126
  54.5 2.0 copy.149
  56.5 10.2 %fusion.19 = bf16[512,8,512]{0,1,2:T(8,128)(2,1)} fusion(bf16[8,512,2,8]{0,3,2,1:T(8,128)(2,1)S(1)} %copy.149, bf16[8,512,2,512]{3,2,1,0:T(2,128)(2,1)} %get-tuple-element.64), kind=kOutput, calls=%fused_computation.23 | convolution fusion | flops 69206016 | bytes 12713984 | tf_op jit(solution)/shard_map/tcrq,tcri->iqc/dot_general | solution.py:133
  66.7 8.6 %copy.151 = bf16[512,8,512]{2,1,0:T(8,128)(2,1)} copy(bf16[512,8,512]{0,1,2:T(8,128)(2,1)} %fusion.19) | data formatting | bytes 8388608 | tf_op jit(solution)/shard_map/convert_element_type | solution.py:135
  75.6 0.7 broadcast_multiply_fusion.2
  76.3 14.4 %fusion.30 = bf16[1024,1024]{1,0:T(8,128)(2,1)S(1)} fusion(f32[1024]{0:T(1024)S(1)} %get-tuple-element.86, f32[1024]{0:T(1024)S(1)} %get-tuple-element.87), kind=kLoop, calls=%fused_computation.27 | loop fusion | flops 5242880 | bytes 2105344 | tf_op jit(solution)/shard_map/while/body/eval_jaxpr/neg | solution.py:96
  90.7 17.0 %fusion.17 = (bf16[1024,1024]{1,0:T(8,128)(2,1)}, bf16[1024,1024]{1,0:T(8,128)(2,1)}) fusion(f32[1024]{0:T(1024)S(1)} %get-tuple-element.86, f32[1024]{0:T(1024)S(1)} %get-tuple-element.87), kind=kLoop, calls=%fused_computation.21 | loop fusion | flops 3145728 | bytes 4202496 | tf_op jit(solution)/shard_map/while/body/eval_jaxpr/convert_element_type | solution.py:20
  107.8 22.0 %reduce-scatter.4.cloned.1.call-done = bf16[32,8,512]{2,1,0:T(8,128)(2,1)} async-done(((bf16[512,8,512]{2,1,0:T(8,128)(2,1)}), bf16[32,8,512]{2,1,0:T(8,128)(2,1)}) %reduce-scatter.4.cloned.1.call-update) | async-done | bytes 262160 | tf_op jit(solution)/shard_map/reduce_scatter | solution.py:136
  129.8 81.1 %reduce-scatter.6.cloned.1.call-done = bf16[32,8,512]{2,1,0:T(8,128)(2,1)} async-done(((bf16[512,8,512]{2,1,0:T(8,128)(2,1)}), bf16[32,8,512]{2,1,0:T(8,128)(2,1)}) %reduce-scatter.6.cloned.1.call-update) | async-done | bytes 262160 | tf_op jit(solution)/shard_map/reduce_scatter | solution.py:136
  210.9 1.1 pad_maximum_fusion
  212.2 1.1 fusion.56
  214.2 13.0 %psum.7 = f32[16,2,8]{0,1,2:T(2,128)S(1)} all-reduce(f32[16,2,8]{0,1,2:T(2,128)S(1)} %constant_dynamic-update-slice_fusion), channel_id=1, replica_groups=mesh['chan'=8,'tm'=16] {'chan'}, use_global_device_ids=true, to_apply=%region_11.0 | all-reduce | flops 256 | bytes 2048 | tf_op jit(solution)/shard_map/psum | solution.py:154
  227.3 22.6 %all_gather.3 = f32[256,2,8]{2,1,0:T(2,128)S(1)} all-gather(f32[16,2,8]{2,1,0:T(2,128)S(1)} %copy.174), channel_id=1, replica_groups=mesh['chan'=8,'tm'=16] {'tm'}, dimensions={0}, use_global_device_ids=true | all-gather | bytes 17408 | tf_op jit(solution)/shard_map/all_gather | solution.py:153
  253.2 12.4 %fusion = f32[32,2048]{1,0:T(8,128)S(1)} fusion(bf16[1024,1024]{1,0:T(8,128)(2,1)} %get-tuple-element.81, bf16[1024,1024]{1,0:T(8,128)(2,1)} %get-tuple-element.80, bf16[1024,1024]{1,0:T(8,128)(2,1)S(1)} %fusion.30, bf16[32,1024]{1,0:T(8,128)(2,1)S(1)} %multiply_convert_fusion, bf16[32,1024]{1,0:T(8,128)(2,1)S(1)} %multiply_convert_fusion.1), kind=kOutput, calls=%fused_computation | convolution fusion | flops 302252032 | bytes 6684672 | tf_op jit(solution)/shard_map/while/body/eval_jaxpr/dot_general | solution.py:98
  265.6 0.7 reshape_reshape.7
  266.5 0.6 pad_maximum_fusion.3
  267.1 26.6 %reduce-scatter.8.cloned.1.call-done = f32[1,8,1024]{2,1,0:T(8,128)} async-done(((f32[8,8,1024]{2,1,0:T(8,128)}), f32[1,8,1024]{2,1,0:T(8,128)}) %reduce-scatter.8.cloned.1.call-update) | async-done | bytes 32784 | tf_op jit(solution)/shard_map/reduce_scatter | solution.py:148
  293.7 0.8 broadcast_multiply_fusion
  294.5 0.6 reshape.231
  (70 shorter events, 5.6 us)
Async XLA Ops:
  7.2 14.3 %copy-start = (s32[2]{0:T(128)S(1)}, s32[2]{0:T(128)}, u32[]{:S(2)}) copy-start(s32[2]{0:T(128)} %param.4) | copy-start | bytes 28
  7.2 122.6 %reduce-scatter.4.cloned.1.call-start = ((), (), s32[]{:S(2)}) async-start(), calls=%async_computation.3 | async-start | bytes 4456448 | tf_op jit(solution)/shard_map/reduce_scatter | solution.py:136
  48.4 162.5 %reduce-scatter.6.cloned.1.call-start = ((), (), s32[]{:S(2)}) async-start(), calls=%async_computation.4 | async-start | bytes 4456448 | tf_op jit(solution)/shard_map/reduce_scatter | solution.py:136
  75.4 218.4 %reduce-scatter.8.cloned.1.call-start = ((), (), s32[]{:S(2)}) async-start(), calls=%async_computation.5 | async-start | bytes 294912 | tf_op jit(solution)/shard_map/reduce_scatter | solution.py:148
Sparse Core Ops, SparseCore 0:
  48.5 81.2 reduce-scatter.3
  133.1 77.7 reduce-scatter.5
  266.4 27.2 reduce-scatter.7

commit v7 on v5

--- a/solution.py
+++ b/solution.py
@@ -3,7 +3,7 @@
 import jax
 import jax.numpy as jnp
 from jax import lax
-from jax.sharding import PartitionSpec as P
+from jax.sharding import Mesh, PartitionSpec as P
 
 CHANNELS = 8192
 DEPTH = 1024
@@ -106,7 +106,7 @@
 
 
 def per_device(voltages, window_stations, channel_flags):
-    tm_size = lax.axis_size("tm")
+    tm_size = lax.axis_size(("tm_major", "tm_minor"))
     chan_size = lax.axis_size("chan")
     inputs = voltages.shape[3]
     stations = inputs // 2
@@ -129,14 +129,15 @@
         "tcrq,tcri->iqc", left, voltages, preferred_element_type=jnp.float32
     ).astype(jnp.bfloat16)
     partial_shape = (inputs, 2, 2 * window, channel_count)
-    summed = lax.psum_scatter(
-        partial,
-        "tm",
-        scatter_dimension=0,
-        tiled=True,
-    ).reshape(-1, *partial_shape[1:])
+    major = lax.axis_size("tm_major")
+    minor = lax.axis_size("tm_minor")
+    partial = partial.reshape(major, minor, -1, *partial.shape[1:])
+    partial = jnp.swapaxes(partial, 0, 1).reshape(-1, *partial.shape[3:])
+    summed = lax.psum_scatter(partial, "tm_minor", scatter_dimension=0, tiled=True)
+    summed = lax.psum_scatter(summed, "tm_major", scatter_dimension=0, tiled=True)
+    summed = summed.reshape(-1, *partial_shape[1:])
     chan_index = lax.axis_index("chan")
-    tm_index = lax.axis_index("tm")
+    tm_index = lax.axis_index(("tm_major", "tm_minor"))
     first_channel = chan_index * channel_count
     local_flags = lax.dynamic_slice_in_dim(channel_flags, first_channel, channel_count, 0)
     spectrum, baseline_stats = spectrum_terms(
@@ -151,7 +152,7 @@
     own_pairs = block_pairs // chan_size
     rm_spectrum = (spectrum * norm_factor).reshape(1, own_pairs, window, 2, DEPTH)
     all_stats = lax.all_gather(
-        lax.psum(baseline_stats, "chan"), "tm", axis=0, tiled=True
+        lax.psum(baseline_stats, "chan"), ("tm_major", "tm_minor"), axis=0, tiled=True
     ) / CHANNELS
     station_axis = jnp.arange(stations, dtype=jnp.int32)
     window_map = (window_stations[:, None] == station_axis[None, :]).astype(jnp.float32)
@@ -169,10 +170,19 @@
 
 
 def solution(mesh):
+    chan_size, tm_size = mesh.devices.shape
+    minor = math.isqrt(tm_size)
+    if minor * minor != tm_size:
+        minor = 1
+    split_mesh = Mesh(
+        mesh.devices.reshape(chan_size, tm_size // minor, minor),
+        ("chan", "tm_major", "tm_minor"),
+    )
+    tm = ("tm_major", "tm_minor")
     return jax.shard_map(
         per_device,
-        mesh=mesh,
-        in_specs=(P("tm", "chan", None, None), P(), P()),
-        out_specs=(P("tm", "chan", None, None, None), P()),
+        mesh=split_mesh,
+        in_specs=(P(tm, "chan", None, None), P(), P()),
+        out_specs=(P(tm, "chan", None, None, None), P()),
         check_vma=False,
     )

time: 237 us -> 275 us (1.16)
  waiting for transfers between devices: 82.9 us -> 110 us
  local copies, waits for them, and re-layouts: 22.9 us -> 31.4 us
    reduce_scatter x1 -> x2, waiting for transfers between devices: 56.4 us -> 83.2 us  [the longest x1 83.1 us: per_device(): lax.psum_scatter(partial, 'tm_minor', scatter_dimension=0, tiled=True)]
    transpose x0 -> x1, local copies, waits for them, and re-layouts: none -> 7.95 us  [per_device(): partial = jnp.swapaxes(partial, 0, 1).reshape(-1, *partial.shape[3:])]
  transfers between devices with their start and end apart: 2 -> 3, of which waited for: 2 -> 2; matrix products, arithmetic and copies ran while one was open for 14% -> 12% of each run, Pallas kernels for 0% -> 0%
where the time goes in v7:
time: 275 us
  waiting for transfers between devices  110 us (40%)
  matrix products  42.2 us (15%)
  other arithmetic  38.9 us (14%)
  blocking collectives  38.4 us (14%)
  local copies, waits for them, and re-layouts  31.4 us (11%)
  between operations  14 us (5%)
    reduce_scatter x1, waiting for transfers between devices, per_device(): lax.psum_scatter(partial, 'tm_minor', scatter_dimension=0, tiled=True)  83.1 us
    reduce_scatter x1, waiting for transfers between devices, per_device(): lax.psum_scatter(spectrum.reshape(block_pairs // 2, -1, DEPTH), 'chan', s...  26.3 us
    all_gather x1, blocking collectives, per_device(): lax.all_gather(lax.psum(baseline_stats, 'chan'), ('tm_major', 'tm_minor')...  23.6 us
    dot_general x1, matrix products, per_device(): jnp.einsum('tcrq,tcri->iqc', left, voltages, preferred_element_type=jnp.f...  19.2 us
    convert_element_type x1, other arithmetic, phase_table(): jnp.sin(angles).astype(jnp.bfloat16)  17 us
    psum x1, blocking collectives, per_device(): lax.psum(baseline_stats, 'chan')  14.7 us
    neg x1, other arithmetic, add_block(): -sine_part  14.4 us
    convert_element_type x1, local copies, waits for them, and re-layouts, per_device(): partial = jnp.einsum('tcrq,tcri->iqc', left, voltages, preferred_element_...  13.7 us
  transfers between devices with their start and end apart: 3, of which 2 were waited for; matrix products, arithmetic and copies ran while one was open for 12% of the time, Pallas kernels for 0%

profile of v7, /device:TPU:0, one launch (start us, length us, event | category | flops | bytes accessed | tf_op | source)
XLA Modules:
  0.0 274.6 jit_solution(345882699281331466)
XLA Ops:
  7.2 0.7 broadcast_multiply_fusion.3
  8.0 10.4 %fusion.17 = bf16[4,8,1024,2]{2,0,3,1:T(4,128)(2,1)S(1)} fusion(bf16[8,1024,2,512]{3,2,1,0:T(2,128)(2,1)} %param.3, s32[4]{0:T(128)S(1)} %add.257), kind=kOutput, calls=%fused_computation.18 | convolution fusion | flops 67176448 | bytes 16908304 | tf_op jit(solution)/shard_map/tcri,iw->tcrw/dot_general | solution.py:121
  19.0 4.7 %copy.83 = bf16[8,1024,2,8]{0,3,2,1:T(8,128)(2,1)} copy(bf16[8,1024,2,8]{1,0,3,2:T(8,128)(2,1)S(1)} %bitcast.185) | data formatting | bytes 524288 | tf_op jit(solution)/shard_map/reshape | solution.py:127
  23.7 19.2 %fusion.4 = bf16[512,8,1024]{0,1,2:T(8,128)(2,1)} fusion(bf16[8,1024,2,8]{0,3,2,1:T(8,128)(2,1)} %copy.83, bf16[8,1024,2,512]{3,2,1,0:T(2,128)(2,1)} %param.3), kind=kOutput, calls=%fused_computation.5 | convolution fusion | flops 138412032 | bytes 25427968 | tf_op jit(solution)/shard_map/tcrq,tcri->iqc/dot_general | solution.py:128
  42.9 13.7 %copy.85 = bf16[512,8,1024]{2,1,0:T(8,128)(2,1)} copy(bf16[512,8,1024]{0,1,2:T(8,128)(2,1)} %fusion.4) | data formatting | bytes 16777216 | tf_op jit(solution)/shard_map/convert_element_type | solution.py:130
  56.6 7.9 %copy.86 = bf16[4,4,32,8,1024]{4,3,2,1,0:T(8,128)(2,1)} copy(bf16[4,4,32,8,1024]{4,3,2,0,1:T(8,128)(2,1)} %bitcast.182) | data formatting | bytes 16777216 | tf_op jit(solution)/shard_map/transpose | solution.py:135
  64.6 83.1 %reduce-scatter.4.cloned.1.call-done = bf16[128,8,1024]{2,1,0:T(8,128)(2,1)} async-done(((bf16[512,8,1024]{2,1,0:T(8,128)(2,1)}), bf16[128,8,1024]{2,1,0:T(8,128)(2,1)}) %reduce-scatter.4.cloned.1.call-update) | async-done | bytes 2097168 | tf_op jit(solution)/shard_map/reduce_scatter | solution.py:136
  147.8 0.7 broadcast_multiply_fusion.2
  148.5 14.4 %fusion.20 = bf16[1024,1024]{1,0:T(8,128)(2,1)S(1)} fusion(f32[1024]{0:T(1024)S(1)} %get-tuple-element.82, f32[1024]{0:T(1024)S(1)} %get-tuple-element.83), kind=kLoop, calls=%fused_computation.19 | loop fusion | flops 5242880 | bytes 2105344 | tf_op jit(solution)/shard_map/while/body/eval_jaxpr/neg | solution.py:95
  162.9 17.0 %fusion.16 = (bf16[1024,1024]{1,0:T(8,128)(2,1)}, bf16[1024,1024]{1,0:T(8,128)(2,1)}) fusion(f32[1024]{0:T(1024)S(1)} %get-tuple-element.82, f32[1024]{0:T(1024)S(1)} %get-tuple-element.83), kind=kLoop, calls=%fused_computation.17 | loop fusion | flops 3145728 | bytes 4202496 | tf_op jit(solution)/shard_map/while/body/eval_jaxpr/convert_element_type | solution.py:19
  180.0 1.2 reshape_reshape.6
  181.2 1.1 fusion.43
  182.4 0.3 fusion.29
  182.6 0.3 fusion.27
  182.9 1.0 fusion.33
  184.6 14.7 %psum.7 = f32[16,2,8]{0,1,2:T(2,128)S(1)} all-reduce(f32[16,2,8]{0,1,2:T(2,128)S(1)} %constant_dynamic-update-slice_fusion), channel_id=1, replica_groups=mesh['chan'=8,'tm_major'=4,'tm_minor'=4] {'chan'}, use_global_device_ids=true, to_apply=%region_11.0 | all-reduce | flops 256 | bytes 2048 | tf_op jit(solution)/shard_map/psum | solution.py:155
  199.4 23.6 %all_gather.3 = f32[256,2,8]{2,1,0:T(2,128)S(1)} all-gather(f32[16,2,8]{2,1,0:T(2,128)S(1)} %copy.99), channel_id=1, replica_groups=mesh['chan'=8,'tm_major'=4,'tm_minor'=4] {'tm_major','tm_minor'}, dimensions={0}, use_global_device_ids=true | all-gather | bytes 17408 | tf_op jit(solution)/shard_map/all_gather | solution.py:154
  225.6 0.3 fusion.23
  226.1 12.6 %fusion.5 = f32[32,2048]{1,0:T(8,128)S(1)} fusion(bf16[1024,1024]{1,0:T(8,128)(2,1)} %get-tuple-element.77, bf16[1024,1024]{1,0:T(8,128)(2,1)} %get-tuple-element.76, bf16[1024,1024]{1,0:T(8,128)(2,1)S(1)} %fusion.20, bf16[32,1024]{1,0:T(8,128)(2,1)S(1)} %multiply_convert_fusion, bf16[32,1024]{1,0:T(8,128)(2,1)S(1)} %multiply_convert_fusion.1), kind=kOutput, calls=%fused_computation.6 | convolution fusion | flops 302252032 | bytes 6684672 | tf_op jit(solution)/shard_map/while/body/eval_jaxpr/dot_general | solution.py:97
  238.7 0.7 reshape_reshape.7
  239.7 0.6 pad_maximum_fusion.1
  240.3 26.3 %reduce-scatter.8.cloned.1.call-done = f32[1,8,1024]{2,1,0:T(8,128)} async-done(((f32[8,8,1024]{2,1,0:T(8,128)}), f32[1,8,1024]{2,1,0:T(8,128)}) %reduce-scatter.8.cloned.1.call-update) | async-done | bytes 32784 | tf_op jit(solution)/shard_map/reduce_scatter | solution.py:149
  266.6 0.8 broadcast_multiply_fusion
  267.4 0.6 reshape.235
  (66 shorter events, 4.5 us)
Async XLA Ops:
  7.2 140.6 %reduce-scatter.4.cloned.1.call-start = ((), (), s32[]{:S(2)}) async-start(), calls=%async_computation.3 | async-start | bytes 10485760 | tf_op jit(solution)/shard_map/reduce_scatter | solution.py:136
  64.6 115.4 %reduce-scatter.6.cloned.1.call-start = ((), (), s32[]{:S(2)}) async-start(), calls=%async_computation.4 | async-start | bytes 2621440 | tf_op jit(solution)/shard_map/reduce_scatter | solution.py:137
  147.8 118.9 %reduce-scatter.8.cloned.1.call-start = ((), (), s32[]{:S(2)}) async-start(), calls=%async_computation.5 | async-start | bytes 294912 | tf_op jit(solution)/shard_map/reduce_scatter | solution.py:149
  180.0 43.9 %copy-start = (s32[2]{0:T(128)S(1)}, s32[2]{0:T(128)}, u32[]{:S(2)}) copy-start(s32[2]{0:T(128)} %param.4) | copy-start | bytes 28
Sparse Core Ops, SparseCore 0:
  64.7 83.0 reduce-scatter.3
  150.2 29.6 reduce-scatter.5
  239.6 26.9 reduce-scatter.7

commit v8 on v5

--- a/solution.py
+++ b/solution.py
@@ -150,8 +150,11 @@
     )
     own_pairs = block_pairs // chan_size
     rm_spectrum = (spectrum * norm_factor).reshape(1, own_pairs, window, 2, DEPTH)
-    all_stats = lax.all_gather(
-        lax.psum(baseline_stats, "chan"), "tm", axis=0, tiled=True
+    chan_stats = lax.psum(baseline_stats, "chan").reshape(1, -1)
+    padded = jnp.pad(chan_stats, ((0, 31), (0, (-chan_stats.shape[1]) % 128)))
+    gathered = lax.all_gather(padded, "tm", axis=0, tiled=False)
+    all_stats = gathered[:, 0, : chan_stats.shape[1]].reshape(
+        stations, window, 8
     ) / CHANNELS
     station_axis = jnp.arange(stations, dtype=jnp.int32)
     window_map = (window_stations[:, None] == station_axis[None, :]).astype(jnp.float32)

time: 237 us -> 250 us (1.055)
  local copies, waits for them, and re-layouts: 22.9 us -> 29.6 us
  other arithmetic: 38.1 us -> 43.4 us
    slice x0 -> x7, local copies, waits for them, and re-layouts: none -> 5.47 us  [the longest x6 5.46 us: per_device(): fields = [all_stats[:, :, column] for column in range(8)]]
    reduce_sum x1, other arithmetic: 0.12 us -> 4.53 us  [station_terms(): jnp.sum(fields[7], 1)[:, None]]
  transfers between devices with their start and end apart: 2 -> 2, of which waited for: 2 -> 2; matrix products, arithmetic and copies ran while one was open for 14% -> 13% of each run, Pallas kernels for 0% -> 0%
where the time goes in v8:
time: 250 us; the launch traced here: 249 us
  waiting for transfers between devices  83.1 us (33%)
  other arithmetic  43.4 us (17%)
  matrix products  42.2 us (17%)
  blocking collectives  36.4 us (15%)
  local copies, waits for them, and re-layouts  29.6 us (12%)
  between operations  14.3 us (6%)
    reduce_scatter x1, waiting for transfers between devices, per_device(): lax.psum_scatter(partial, 'tm', scatter_dimension=0, tiled=True)  56.8 us
    reduce_scatter x1, waiting for transfers between devices, per_device(): lax.psum_scatter(spectrum.reshape(block_pairs // 2, -1, DEPTH), 'chan', s...  26.3 us
    all_gather x1, blocking collectives, per_device(): gathered = lax.all_gather(padded, 'tm', axis=0, tiled=False)  23.3 us
    dot_general x1, matrix products, per_device(): jnp.einsum('tcrq,tcri->iqc', left, voltages, preferred_element_type=jnp.f...  19.2 us
    convert_element_type x1, other arithmetic, phase_table(): jnp.sin(angles).astype(jnp.bfloat16)  17 us
    neg x1, other arithmetic, add_block(): -sine_part  14.4 us
    convert_element_type x1, local copies, waits for them, and re-layouts, per_device(): partial = jnp.einsum('tcrq,tcri->iqc', left, voltages, preferred_element_...  13.6 us
    psum x1, blocking collectives, per_device(): chan_stats = lax.psum(baseline_stats, 'chan').reshape(1, -1)  13.1 us
  transfers between devices with their start and end apart: 2, of which 2 were waited for; matrix products, arithmetic and copies ran while one was open for 13% of the time, Pallas kernels for 0%

profile of v8, /device:TPU:0, one launch (start us, length us, event | category | flops | bytes accessed | tf_op | source)
XLA Modules:
  0.0 249.2 jit_solution(15920987627054459650)
XLA Ops:
  7.2 0.7 broadcast_multiply_fusion.2
  8.0 10.4 %fusion.17 = bf16[4,8,1024,2]{2,0,3,1:T(4,128)(2,1)S(1)} fusion(bf16[8,1024,2,512]{3,2,1,0:T(2,128)(2,1)} %param.3, s32[4]{0:T(128)S(1)} %add.257), kind=kOutput, calls=%fused_computation.18 | convolution fusion | flops 67176448 | bytes 16908304 | tf_op jit(solution)/shard_map/tcri,iw->tcrw/dot_general | solution.py:121
  19.0 4.7 %copy.288 = bf16[8,1024,2,8]{0,3,2,1:T(8,128)(2,1)} copy(bf16[8,1024,2,8]{1,0,3,2:T(8,128)(2,1)S(1)} %bitcast.234) | data formatting | bytes 524288 | tf_op jit(solution)/shard_map/reshape | solution.py:127
  23.7 19.2 %fusion.4 = bf16[512,8,1024]{0,1,2:T(8,128)(2,1)} fusion(bf16[8,1024,2,8]{0,3,2,1:T(8,128)(2,1)} %copy.288, bf16[8,1024,2,512]{3,2,1,0:T(2,128)(2,1)} %param.3), kind=kOutput, calls=%fused_computation.5 | convolution fusion | flops 138412032 | bytes 25427968 | tf_op jit(solution)/shard_map/tcrq,tcri->iqc/dot_general | solution.py:128
  42.9 13.6 %copy.290 = bf16[512,8,1024]{2,1,0:T(8,128)(2,1)} copy(bf16[512,8,1024]{0,1,2:T(8,128)(2,1)} %fusion.4) | data formatting | bytes 16777216 | tf_op jit(solution)/shard_map/convert_element_type | solution.py:130
  56.6 0.7 broadcast_multiply_fusion.1
  57.3 14.4 %fusion.20 = bf16[1024,1024]{1,0:T(8,128)(2,1)S(1)} fusion(f32[1024]{0:T(1024)S(1)} %get-tuple-element.88, f32[1024]{0:T(1024)S(1)} %get-tuple-element.89), kind=kLoop, calls=%fused_computation.19 | loop fusion | flops 5242880 | bytes 2105344 | tf_op jit(solution)/shard_map/while/body/eval_jaxpr/neg | solution.py:95
  71.7 17.0 %fusion.16 = (bf16[1024,1024]{1,0:T(8,128)(2,1)}, bf16[1024,1024]{1,0:T(8,128)(2,1)}) fusion(f32[1024]{0:T(1024)S(1)} %get-tuple-element.88, f32[1024]{0:T(1024)S(1)} %get-tuple-element.89), kind=kLoop, calls=%fused_computation.17 | loop fusion | flops 3145728 | bytes 4202496 | tf_op jit(solution)/shard_map/while/body/eval_jaxpr/convert_element_type | solution.py:19
  88.7 56.8 %reduce-scatter.3.cloned.1.call-done = bf16[32,8,1024]{2,1,0:T(8,128)(2,1)} async-done(((bf16[512,8,1024]{2,1,0:T(8,128)(2,1)}), bf16[32,8,1024]{2,1,0:T(8,128)(2,1)}) %reduce-scatter.3.cloned.1.call-update) | async-done | bytes 524304 | tf_op jit(solution)/shard_map/reduce_scatter | solution.py:132
  145.5 1.2 reshape_reshape.6
  146.7 1.9 fusion.66
  149.6 13.1 %psum.7 = f32[1,256]{1,0:T(1,128)S(1)} all-reduce(f32[1,256]{1,0:T(1,128)S(1)} %reshape.233), channel_id=1, replica_groups=mesh['chan'=8,'tm'=16] {'chan'}, use_global_device_ids=true, to_apply=%region_10.0 | all-reduce | flops 256 | bytes 2048 | tf_op jit(solution)/shard_map/psum | solution.py:153
  162.8 23.3 %all-gather = f32[512,256]{1,0:T(8,128)S(1)} all-gather(f32[32,256]{1,0:T(8,128)S(1)} %pad.4), channel_id=2, replica_groups=mesh['chan'=8,'tm'=16] {'tm'}, dimensions={0}, use_global_device_ids=true | all-gather | bytes 557056 | tf_op jit(solution)/shard_map/all_gather | solution.py:155
  186.5 4.5 %slice_reduce_fusion = (f32[256]{0:T(256)S(1)}, f32[2]{0:T(128)S(1)}, f32[256,2,1]{2,1,0:T(2,128)}, f32[256,2,1]{2,1,0:T(2,128)S(1)}, f32[256,2,1]{2,1,0:T(2,128...) fusion(f32[256,2,8]{2,1,0:T(2,128)S(1)} %div.78), kind=kLoop, calls=%fused_computation.20 | loop fusion | flops 766 | bytes 29704 | tf_op jit(solution)/shard_map/reduce_sum | solution.py:38
  191.0 1.1 copy.315
  192.1 1.1 copy.316
  193.2 1.1 copy.317
  194.2 1.1 copy.318
  195.3 1.1 copy.319
  198.8 1.1 fusion.27
  200.4 12.6 %fusion.5 = f32[32,2048]{1,0:T(8,128)S(1)} fusion(bf16[1024,1024]{1,0:T(8,128)(2,1)} %get-tuple-element.83, bf16[1024,1024]{1,0:T(8,128)(2,1)} %get-tuple-element.82, bf16[1024,1024]{1,0:T(8,128)(2,1)S(1)} %fusion.20, bf16[32,1024]{1,0:T(8,128)(2,1)S(1)} %multiply_convert_fusion, bf16[32,1024]{1,0:T(8,128)(2,1)S(1)} %multiply_convert_fusion.1), kind=kOutput, calls=%fused_computation.6 | convolution fusion | flops 302252032 | bytes 6684672 | tf_op jit(solution)/shard_map/while/body/eval_jaxpr/dot_general | solution.py:97
  213.0 0.7 reshape_reshape.7
  214.6 26.3 %reduce-scatter.5.cloned.1.call-done = f32[1,8,1024]{2,1,0:T(8,128)} async-done(((f32[8,8,1024]{2,1,0:T(8,128)}), f32[1,8,1024]{2,1,0:T(8,128)}) %reduce-scatter.5.cloned.1.call-update) | async-done | bytes 32784 | tf_op jit(solution)/shard_map/reduce_scatter | solution.py:148
  240.9 0.8 broadcast_multiply_fusion
  (66 shorter events, 6.5 us)
Async XLA Ops:
  7.2 138.3 %reduce-scatter.3.cloned.1.call-start = ((), (), s32[]{:S(2)}) async-start(), calls=%async_computation.2 | async-start | bytes 8912896 | tf_op jit(solution)/shard_map/reduce_scatter | solution.py:132
  56.5 184.4 %reduce-scatter.5.cloned.1.call-start = ((), (), s32[]{:S(2)}) async-start(), calls=%async_computation.3 | async-start | bytes 294912 | tf_op jit(solution)/shard_map/reduce_scatter | solution.py:148
  148.8 48.3 %copy-start = (s32[2]{0:T(128)S(1)}, s32[2]{0:T(128)}, u32[]{:S(2)}) copy-start(s32[2]{0:T(128)} %param.4) | copy-start | bytes 28
Sparse Core Ops, SparseCore 0:
  56.6 88.7 reduce-scatter.2
  213.9 26.9 reduce-scatter.4

commit v9 on v8

--- a/solution.py
+++ b/solution.py
@@ -151,7 +151,7 @@
     own_pairs = block_pairs // chan_size
     rm_spectrum = (spectrum * norm_factor).reshape(1, own_pairs, window, 2, DEPTH)
     chan_stats = lax.psum(baseline_stats, "chan").reshape(1, -1)
-    padded = jnp.pad(chan_stats, ((0, 31), (0, (-chan_stats.shape[1]) % 128)))
+    padded = jnp.pad(chan_stats, ((0, 63), (0, (-chan_stats.shape[1]) % 128)))
     gathered = lax.all_gather(padded, "tm", axis=0, tiled=False)
     all_stats = gathered[:, 0, : chan_stats.shape[1]].reshape(
         stations, window, 8

time: 250 us -> 252 us (level)
  waiting for transfers between devices: 83.1 us -> 115 us
  blocking collectives: 36.4 us -> 13.1 us
  local copies, waits for them, and re-layouts: 29.6 us -> 25.7 us
    all_gather x0 -> x1, waiting for transfers between devices: none -> 42.3 us  [per_device(): gathered = lax.all_gather(padded, 'tm', axis=0, tiled=False)]
    all_gather x1 -> x0, blocking collectives: 23.3 us -> none  [per_device(): gathered = lax.all_gather(padded, 'tm', axis=0, tiled=False)]
    reduce_scatter x1, waiting for transfers between devices: 26.3 us -> 16.1 us  [per_device(): lax.psum_scatter(spectrum.reshape(block_pairs // 2, -1, DEPTH), 'chan', s...]
    slice x6, local copies, waits for them, and re-layouts: 5.46 us -> 0.76 us  [per_device(): fields = [all_stats[:, :, column] for column in range(8)]]
  transfers between devices with their start and end apart: 2 -> 3, of which waited for: 2 -> 3; matrix products, arithmetic and copies ran while one was open for 13% -> 14% of each run, Pallas kernels for 0% -> 0%
where the time goes in v9:
time: 252 us
  waiting for transfers between devices  115 us (46%)
  matrix products  42 us (17%)
  other arithmetic  41.6 us (17%)
  local copies, waits for them, and re-layouts  25.7 us (10%)
  between operations  14 us (6%)
  blocking collectives  13.1 us (5%)
    reduce_scatter x1, waiting for transfers between devices, per_device(): lax.psum_scatter(partial, 'tm', scatter_dimension=0, tiled=True)  56.8 us
    all_gather x1, waiting for transfers between devices, per_device(): gathered = lax.all_gather(padded, 'tm', axis=0, tiled=False)  42.3 us
    dot_general x1, matrix products, per_device(): jnp.einsum('tcrq,tcri->iqc', left, voltages, preferred_element_type=jnp.f...  19.2 us
    convert_element_type x1, other arithmetic, phase_table(): jnp.sin(angles).astype(jnp.bfloat16)  17 us
    reduce_scatter x1, waiting for transfers between devices, per_device(): lax.psum_scatter(spectrum.reshape(block_pairs // 2, -1, DEPTH), 'chan', s...  16.1 us
    neg x1, other arithmetic, add_block(): -sine_part  14.4 us
    convert_element_type x1, local copies, waits for them, and re-layouts, per_device(): partial = jnp.einsum('tcrq,tcri->iqc', left, voltages, preferred_element_...  13.6 us
    psum x1, blocking collectives, per_device(): chan_stats = lax.psum(baseline_stats, 'chan').reshape(1, -1)  13.1 us
  transfers between devices with their start and end apart: 3, of which 3 were waited for; matrix products, arithmetic and copies ran while one was open for 14% of the time, Pallas kernels for 0%

profile of v9, /device:TPU:0, one launch (start us, length us, event | category | flops | bytes accessed | tf_op | source)
XLA Modules:
  0.0 251.8 jit_solution(14793821192502915107)
XLA Ops:
  7.2 0.7 broadcast_multiply_fusion.2
  8.0 10.4 %fusion.17 = bf16[4,8,1024,2]{2,0,3,1:T(4,128)(2,1)S(1)} fusion(bf16[8,1024,2,512]{3,2,1,0:T(2,128)(2,1)} %param.3, s32[4]{0:T(128)S(1)} %add.257), kind=kOutput, calls=%fused_computation.18 | convolution fusion | flops 67176448 | bytes 16908304 | tf_op jit(solution)/shard_map/tcri,iw->tcrw/dot_general | solution.py:121
  19.0 4.7 %copy.288 = bf16[8,1024,2,8]{0,3,2,1:T(8,128)(2,1)} copy(bf16[8,1024,2,8]{1,0,3,2:T(8,128)(2,1)S(1)} %bitcast.234) | data formatting | bytes 524288 | tf_op jit(solution)/shard_map/reshape | solution.py:127
  23.7 19.2 %fusion.4 = bf16[512,8,1024]{0,1,2:T(8,128)(2,1)} fusion(bf16[8,1024,2,8]{0,3,2,1:T(8,128)(2,1)} %copy.288, bf16[8,1024,2,512]{3,2,1,0:T(2,128)(2,1)} %param.3), kind=kOutput, calls=%fused_computation.5 | convolution fusion | flops 138412032 | bytes 25427968 | tf_op jit(solution)/shard_map/tcrq,tcri->iqc/dot_general | solution.py:128
  42.9 13.6 %copy.290 = bf16[512,8,1024]{2,1,0:T(8,128)(2,1)} copy(bf16[512,8,1024]{0,1,2:T(8,128)(2,1)} %fusion.4) | data formatting | bytes 16777216 | tf_op jit(solution)/shard_map/convert_element_type | solution.py:130
  56.6 0.7 broadcast_multiply_fusion.1
  57.3 14.4 %fusion.20 = bf16[1024,1024]{1,0:T(8,128)(2,1)S(1)} fusion(f32[1024]{0:T(1024)S(1)} %get-tuple-element.88, f32[1024]{0:T(1024)S(1)} %get-tuple-element.89), kind=kLoop, calls=%fused_computation.19 | loop fusion | flops 5242880 | bytes 2105344 | tf_op jit(solution)/shard_map/while/body/eval_jaxpr/neg | solution.py:95
  71.7 17.0 %fusion.16 = (bf16[1024,1024]{1,0:T(8,128)(2,1)}, bf16[1024,1024]{1,0:T(8,128)(2,1)}) fusion(f32[1024]{0:T(1024)S(1)} %get-tuple-element.88, f32[1024]{0:T(1024)S(1)} %get-tuple-element.89), kind=kLoop, calls=%fused_computation.17 | loop fusion | flops 3145728 | bytes 4202496 | tf_op jit(solution)/shard_map/while/body/eval_jaxpr/convert_element_type | solution.py:19
  88.7 56.8 %reduce-scatter.3.cloned.1.call-done = bf16[32,8,1024]{2,1,0:T(8,128)(2,1)} async-done(((bf16[512,8,1024]{2,1,0:T(8,128)(2,1)}), bf16[32,8,1024]{2,1,0:T(8,128)(2,1)}) %reduce-scatter.3.cloned.1.call-update) | async-done | bytes 524304 | tf_op jit(solution)/shard_map/reduce_scatter | solution.py:132
  145.5 1.2 reshape_reshape.6
  146.7 1.1 fusion.66
  148.0 0.3 fusion.28
  149.3 12.4 %fusion.5 = f32[32,2048]{1,0:T(8,128)S(1)} fusion(bf16[1024,1024]{1,0:T(8,128)(2,1)} %get-tuple-element.83, bf16[1024,1024]{1,0:T(8,128)(2,1)} %get-tuple-element.82, bf16[1024,1024]{1,0:T(8,128)(2,1)S(1)} %fusion.20, bf16[32,1024]{1,0:T(8,128)(2,1)S(1)} %multiply_convert_fusion, bf16[32,1024]{1,0:T(8,128)(2,1)S(1)} %multiply_convert_fusion.1), kind=kOutput, calls=%fused_computation.6 | convolution fusion | flops 302252032 | bytes 6684672 | tf_op jit(solution)/shard_map/while/body/eval_jaxpr/dot_general | solution.py:97
  161.7 0.8 reshape_reshape.7
  162.8 13.1 %psum.7 = f32[1,256]{1,0:T(1,128)S(1)} all-reduce(f32[1,256]{1,0:T(1,128)S(1)} %reshape.233), channel_id=1, replica_groups=mesh['chan'=8,'tm'=16] {'chan'}, use_global_device_ids=true, to_apply=%region_10.0 | all-reduce | flops 256 | bytes 2048 | tf_op jit(solution)/shard_map/psum | solution.py:153
  176.0 0.6 pad.4
  176.6 16.1 %reduce-scatter.5.cloned.1.call-done = f32[1,8,1024]{2,1,0:T(8,128)} async-done(((f32[8,8,1024]{2,1,0:T(8,128)}), f32[1,8,1024]{2,1,0:T(8,128)}) %reduce-scatter.5.cloned.1.call-update) | async-done | bytes 32784 | tf_op jit(solution)/shard_map/reduce_scatter | solution.py:148
  192.8 0.8 broadcast_multiply_fusion
  193.5 0.6 reshape.232
  194.2 42.3 %all-gather.3.cloned.1.call-done = f32[1024,256]{1,0:T(8,128)} async-done(((f32[64,256]{1,0:T(8,128)}), f32[1024,256]{1,0:T(8,128)}) %all-gather.3.cloned.1.call-update) | async-done | bytes 1048592 | tf_op jit(solution)/shard_map/all_gather | solution.py:155
  236.4 0.9 slice.138
  237.4 0.4 div.78
  237.8 3.7 %slice_reduce_fusion = (f32[256]{0:T(256)S(1)}, f32[2]{0:T(128)S(1)}, f32[256,2,1]{2,1,0:T(2,128)S(1)}, f32[256,2,1]{2,1,0:T(2,128)S(1)}, f32[256,2,1]{2,1,0:T(2...) fusion(f32[256,2,8]{2,1,0:T(2,128)S(1)} %div.78), kind=kLoop, calls=%fused_computation.20 | loop fusion | flops 766 | bytes 29704 | tf_op jit(solution)/shard_map/reduce_sum | solution.py:38
  244.7 0.6 pad_maximum_fusion.1
  (68 shorter events, 5.3 us)
Async XLA Ops:
  7.2 138.3 %reduce-scatter.3.cloned.1.call-start = ((), (), s32[]{:S(2)}) async-start(), calls=%async_computation.2 | async-start | bytes 8912896 | tf_op jit(solution)/shard_map/reduce_scatter | solution.py:132
  56.5 136.2 %reduce-scatter.5.cloned.1.call-start = ((), (), s32[]{:S(2)}) async-start(), calls=%async_computation.3 | async-start | bytes 294912 | tf_op jit(solution)/shard_map/reduce_scatter | solution.py:148
  161.7 81.0 %copy-start = (s32[2]{0:T(128)S(1)}, s32[2]{0:T(128)}, u32[]{:S(2)}) copy-start(s32[2]{0:T(128)} %param.4) | copy-start | bytes 28
  162.5 73.9 %all-gather.3.cloned.1.call-start = ((), (), s32[]{:S(2)}) async-start(), calls=%async_computation.4 | async-start | bytes 1114112 | tf_op jit(solution)/shard_map/all_gather | solution.py:155
Sparse Core Ops, SparseCore 0:
  56.6 88.7 reduce-scatter.2
  162.6 30.0 reduce-scatter.4
  194.9 41.4 all-gather.2

commit v10 on v5

--- a/solution.py
+++ b/solution.py
@@ -103,6 +103,31 @@
         jnp.zeros((pairs * window, 2 * DEPTH), jnp.float32),
     )
     return (total.reshape(pairs, window, 2 * DEPTH), baseline_stats)
+
+
+def butterfly_sum(value, axis):
+    size = lax.axis_size(axis)
+    distance = 1
+    while distance < size:
+        pairs = [(index, index ^ distance) for index in range(size)]
+        value = value + lax.ppermute(value, axis, pairs)
+        distance *= 2
+    return value
+
+
+def butterfly_gather(value, axis):
+    size = lax.axis_size(axis)
+    index = lax.axis_index(axis)
+    distance = 1
+    while distance < size:
+        pairs = [(source, source ^ distance) for source in range(size)]
+        other = lax.ppermute(value, axis, pairs)
+        lower = (index & distance) == 0
+        value = jnp.where(
+            lower, jnp.concatenate([value, other], 0), jnp.concatenate([other, value], 0)
+        )
+        distance *= 2
+    return value
 
 
 def per_device(voltages, window_stations, channel_flags):
@@ -150,9 +175,7 @@
     )
     own_pairs = block_pairs // chan_size
     rm_spectrum = (spectrum * norm_factor).reshape(1, own_pairs, window, 2, DEPTH)
-    all_stats = lax.all_gather(
-        lax.psum(baseline_stats, "chan"), "tm", axis=0, tiled=True
-    ) / CHANNELS
+    all_stats = butterfly_gather(butterfly_sum(baseline_stats, "chan"), "tm") / CHANNELS
     station_axis = jnp.arange(stations, dtype=jnp.int32)
     window_map = (window_stations[:, None] == station_axis[None, :]).astype(jnp.float32)
     station_map = jnp.eye(stations, dtype=jnp.float32)

time: 237 us -> 254 us (1.072)
  waiting for transfers between devices: 82.9 us -> 123 us
  blocking collectives: 36.5 us -> 0 us
  starting transfers between devices: 0.08 us -> 12.5 us
    reduce_scatter x1, waiting for transfers between devices: 56.4 us -> 87.8 us  [per_device(): lax.psum_scatter(partial, 'tm', scatter_dimension=0, tiled=True)]
    all_gather x1 -> x0, blocking collectives: 23.1 us -> none  [per_device(): lax.all_gather(lax.psum(baseline_stats, 'chan'), 'tm', axis=0, tiled=True)]
    psum x1 -> x0, blocking collectives: 13.4 us -> none  [per_device(): lax.psum(baseline_stats, 'chan')]
    ppermute x0 -> x7, starting transfers between devices: none -> 12.4 us  [the longest x4 7.93 us: butterfly_gather(): other = lax.ppermute(value, axis, pairs)]
    ppermute x0 -> x7, waiting for transfers between devices: none -> 9.13 us  [the longest x4 6.81 us: butterfly_gather(): other = lax.ppermute(value, axis, pairs)]
  transfers between devices with their start and end apart: 2 -> 9, of which waited for: 2 -> 6; matrix products, arithmetic and copies ran while one was open for 14% -> 20% of each run, Pallas kernels for 0% -> 0%
where the time goes in v10:
time: 254 us
  waiting for transfers between devices  123 us (48%)
  matrix products  41.9 us (16%)
  other arithmetic  38.9 us (15%)
  local copies, waits for them, and re-layouts  22.8 us (9%)
  between operations  14.3 us (6%)
  starting transfers between devices  12.5 us (5%)
    reduce_scatter x1, waiting for transfers between devices, per_device(): lax.psum_scatter(partial, 'tm', scatter_dimension=0, tiled=True)  87.8 us
    reduce_scatter x1, waiting for transfers between devices, per_device(): lax.psum_scatter(spectrum.reshape(block_pairs // 2, -1, DEPTH), 'chan', s...  26.2 us
    dot_general x1, matrix products, per_device(): jnp.einsum('tcrq,tcri->iqc', left, voltages, preferred_element_type=jnp.f...  19.2 us
    convert_element_type x1, other arithmetic, phase_table(): jnp.sin(angles).astype(jnp.bfloat16)  16.9 us
    neg x1, other arithmetic, add_block(): -sine_part  15.1 us
    convert_element_type x1, local copies, waits for them, and re-layouts, per_device(): partial = jnp.einsum('tcrq,tcri->iqc', left, voltages, preferred_element_...  13.7 us
    dot_general x1, matrix products, add_block(): return total + jnp.dot(left, right, preferred_element_type=jnp.float32)  12.3 us
    dot_general x1, matrix products, per_device(): jnp.einsum('tcri,iw->tcrw', voltages, selector, preferred_element_type=jn...  10.4 us
  transfers between devices with their start and end apart: 9, of which 6 were waited for; matrix products, arithmetic and copies ran while one was open for 20% of the time, Pallas kernels for 0%

profile of v10, /device:TPU:0, one launch (start us, length us, event | category | flops | bytes accessed | tf_op | source)
XLA Modules:
  0.0 253.7 jit_solution(11703100344820056367)
XLA Ops:
  8.0 10.4 %fusion.17 = bf16[4,8,1024,2]{2,0,3,1:T(4,128)(2,1)S(1)} fusion(bf16[8,1024,2,512]{3,2,1,0:T(2,128)(2,1)} %param.3, s32[4]{0:T(128)S(1)} %add.262), kind=kOutput, calls=%fused_computation.18 | convolution fusion | flops 67176448 | bytes 16908304 | tf_op jit(solution)/shard_map/tcri,iw->tcrw/dot_general | solution.py:146
  19.0 4.7 %copy.88 = bf16[8,1024,2,8]{0,3,2,1:T(8,128)(2,1)} copy(bf16[8,1024,2,8]{1,0,3,2:T(8,128)(2,1)S(1)} %bitcast.179) | data formatting | bytes 524288 | tf_op jit(solution)/shard_map/reshape | solution.py:152
  23.7 19.2 %fusion.4 = bf16[512,8,1024]{0,1,2:T(8,128)(2,1)} fusion(bf16[8,1024,2,8]{0,3,2,1:T(8,128)(2,1)} %copy.88, bf16[8,1024,2,512]{3,2,1,0:T(2,128)(2,1)} %param.3), kind=kOutput, calls=%fused_computation.5 | convolution fusion | flops 138412032 | bytes 25427968 | tf_op jit(solution)/shard_map/tcrq,tcri->iqc/dot_general | solution.py:153
  42.9 13.7 %copy.90 = bf16[512,8,1024]{2,1,0:T(8,128)(2,1)} copy(bf16[512,8,1024]{0,1,2:T(8,128)(2,1)} %fusion.4) | data formatting | bytes 16777216 | tf_op jit(solution)/shard_map/convert_element_type | solution.py:155
  56.7 0.7 broadcast_multiply_fusion.1
  57.4 87.8 %reduce-scatter.3.cloned.1.call-done = bf16[32,8,1024]{2,1,0:T(8,128)(2,1)} async-done(((bf16[512,8,1024]{2,1,0:T(8,128)(2,1)}), bf16[32,8,1024]{2,1,0:T(8,128)(2,1)}) %reduce-scatter.3.cloned.1.call-update) | async-done | bytes 524304 | tf_op jit(solution)/shard_map/reduce_scatter | solution.py:157
  145.2 1.2 reshape_reshape.6
  146.5 1.1 fusion.44
  148.5 16.9 %fusion.16 = (bf16[1024,1024]{1,0:T(8,128)(2,1)S(1)}, bf16[1024,1024]{1,0:T(8,128)(2,1)}) fusion(f32[1024]{0:T(1024)S(1)} %get-tuple-element.82, f32[1024]{0:T(1024)S(1)} %get-tuple-element.83), kind=kLoop, calls=%fused_computation.17 | loop fusion | flops 3145728 | bytes 4202496 | tf_op jit(solution)/shard_map/while/body/eval_jaxpr/convert_element_type | solution.py:19
  165.5 1.7 collective-permute-start.1
  167.1 15.1 %fusion.20 = bf16[1024,1024]{1,0:T(8,128)(2,1)} fusion(f32[1024]{0:T(1024)S(1)} %get-tuple-element.82, f32[1024]{0:T(1024)S(1)} %get-tuple-element.83), kind=kLoop, calls=%fused_computation.19 | loop fusion | flops 5242880 | bytes 2105344 | tf_op jit(solution)/shard_map/while/body/eval_jaxpr/neg | solution.py:95
  182.2 2.8 %collective-permute-start.2 = (f32[16,2,8]{0,1,2:T(2,128)S(1)}, f32[16,2,8]{0,1,2:T(2,128)S(1)}, u32[]{:S(2)}, u32[]{:S(2)}) collective-permute-start(f32[16,2,8]{0,1,2:T(2,128)S(1)} %add.281), channel_id=1, source_target_pairs={{0,64},{16,80},{32,96},{48,112},{64,0},{80,16},{96,32},{112,48},{1... | collective-permute-start | bytes 3080 | tf_op jit(solution)/shard_map/ppermute | solution.py:113
  185.1 2.3 collective-permute-done.2
  187.5 1.2 collective-permute-start.3
  189.0 2.2 collective-permute-done.3
  191.2 2.8 %collective-permute-start.4 = (f32[32,2,8]{0,1,2:T(2,128)S(1)}, f32[32,2,8]{0,1,2:T(2,128)S(1)}, u32[]{:S(2)}, u32[]{:S(2)}) collective-permute-start(f32[32,2,8]{0,1,2:T(2,128)S(1)} %maximum_select_fusion.1), channel_id=1, source_target_pairs={{0,2},{1,3},{2,0},{3,1},{4,6},{5,7},{6,4},{7,5},{8,10},{9,11},{10,... | collective-permute-start | bytes 6152 | tf_op jit(solution)/shard_map/ppermute | solution.py:124
  194.2 2.2 collective-permute-done.4
  196.5 1.3 collective-permute-start.5
  197.9 2.4 collective-permute-done.5
  200.4 2.6 %collective-permute-start.6 = (f32[128,2,8]{0,1,2:T(2,128)S(1)}, f32[128,2,8]{0,1,2:T(2,128)S(1)}, u32[]{:S(2)}, u32[]{:S(2)}) collective-permute-start(f32[128,2,8]{0,1,2:T(2,128)S(1)} %maximum_select_fusion.3), channel_id=1, source_target_pairs={{0,8},{1,9},{2,10},{3,11},{4,12},{5,13},{6,14},{7,15},{8,0},{9,1},... | collective-permute-start | bytes 24584 | tf_op jit(solution)/shard_map/ppermute | solution.py:124
  203.0 12.3 %fusion.5 = f32[32,2048]{1,0:T(8,128)S(1)} fusion(bf16[1024,1024]{1,0:T(8,128)(2,1)} %get-tuple-element.77, bf16[1024,1024]{1,0:T(8,128)(2,1)S(1)} %get-tuple-element.76, bf16[1024,1024]{1,0:T(8,128)(2,1)} %fusion.20, bf16[32,1024]{1,0:T(8,128)(2,1)S(1)} %multiply_convert_fusion, bf16[32,1024]{1,0:T(8,128)(2,1)S(1)} %multiply_convert_fusion.1), kind=kOutput, calls=%fused_computation.6 | convolution fusion | flops 302252032 | bytes 6684672 | tf_op jit(solution)/shard_map/while/body/eval_jaxpr/dot_general | solution.py:97
  215.3 0.7 reshape_reshape.7
  219.3 26.2 %reduce-scatter.5.cloned.1.call-done = f32[1,8,1024]{2,1,0:T(8,128)} async-done(((f32[8,8,1024]{2,1,0:T(8,128)}), f32[1,8,1024]{2,1,0:T(8,128)}) %reduce-scatter.5.cloned.1.call-update) | async-done | bytes 32784 | tf_op jit(solution)/shard_map/reduce_scatter | solution.py:173
  245.5 0.8 broadcast_multiply_fusion
  (73 shorter events, 7.0 us)
Async XLA Ops:
  7.2 138.1 %reduce-scatter.3.cloned.1.call-start = ((), (), s32[]{:S(2)}) async-start(), calls=%async_computation.2 | async-start | bytes 8912896 | tf_op jit(solution)/shard_map/reduce_scatter | solution.py:157
  56.6 188.9 %reduce-scatter.5.cloned.1.call-start = ((), (), s32[]{:S(2)}) async-start(), calls=%async_computation.3 | async-start | bytes 294912 | tf_op jit(solution)/shard_map/reduce_scatter | solution.py:173
  148.4 17.0 %collective-permute-start = (f32[16,2,8]{0,1,2:T(2,128)S(1)}, f32[16,2,8]{0,1,2:T(2,128)S(1)}, u32[]{:S(2)}, u32[]{:S(2)}) collective-permute-start(f32[16,2,8]{0,1,2:T(2,128)S(1)} %constant_dynamic-update-slice_fusion), channel_id=1, source_target_pairs={{0,16},{16,0},{32,48},{48,32},{64,80},{80,64},{96,112},{112,96},{1... | collective-permute-start | bytes 3080 | tf_op jit(solution)/shard_map/ppermute | solution.py:113
  165.5 16.7 %collective-permute-start.1 = (f32[16,2,8]{0,1,2:T(2,128)S(1)}, f32[16,2,8]{0,1,2:T(2,128)S(1)}, u32[]{:S(2)}, u32[]{:S(2)}) collective-permute-start(f32[16,2,8]{0,1,2:T(2,128)S(1)} %add.280), channel_id=1, source_target_pairs={{0,32},{16,48},{32,0},{48,16},{64,96},{80,112},{96,64},{112,80},{1... | collective-permute-start | bytes 3080 | tf_op jit(solution)/shard_map/ppermute | solution.py:113
  182.2 5.2 %collective-permute-start.2 = (f32[16,2,8]{0,1,2:T(2,128)S(1)}, f32[16,2,8]{0,1,2:T(2,128)S(1)}, u32[]{:S(2)}, u32[]{:S(2)}) collective-permute-start(f32[16,2,8]{0,1,2:T(2,128)S(1)} %add.281), channel_id=1, source_target_pairs={{0,64},{16,80},{32,96},{48,112},{64,0},{80,16},{96,32},{112,48},{1... | collective-permute-start | bytes 3080 | tf_op jit(solution)/shard_map/ppermute | solution.py:113
  187.5 3.7 %collective-permute-start.3 = (f32[16,2,8]{0,1,2:T(2,128)S(1)}, f32[16,2,8]{0,1,2:T(2,128)S(1)}, u32[]{:S(2)}, u32[]{:S(2)}) collective-permute-start(f32[16,2,8]{0,1,2:T(2,128)S(1)} %add.282), channel_id=1, source_target_pairs={{0,1},{1,0},{2,3},{3,2},{4,5},{5,4},{6,7},{7,6},{8,9},{9,8},{10,11... | collective-permute-start | bytes 3080 | tf_op jit(solution)/shard_map/ppermute | solution.py:124
  191.2 5.2 %collective-permute-start.4 = (f32[32,2,8]{0,1,2:T(2,128)S(1)}, f32[32,2,8]{0,1,2:T(2,128)S(1)}, u32[]{:S(2)}, u32[]{:S(2)}) collective-permute-start(f32[32,2,8]{0,1,2:T(2,128)S(1)} %maximum_select_fusion.1), channel_id=1, source_target_pairs={{0,2},{1,3},{2,0},{3,1},{4,6},{5,7},{6,4},{7,5},{8,10},{9,11},{10,... | collective-permute-start | bytes 6152 | tf_op jit(solution)/shard_map/ppermute | solution.py:124
  196.5 3.8 %collective-permute-start.5 = (f32[64,2,8]{0,1,2:T(2,128)S(1)}, f32[64,2,8]{0,1,2:T(2,128)S(1)}, u32[]{:S(2)}, u32[]{:S(2)}) collective-permute-start(f32[64,2,8]{0,1,2:T(2,128)S(1)} %maximum_select_fusion.2), channel_id=1, source_target_pairs={{0,4},{1,5},{2,6},{3,7},{4,0},{5,1},{6,2},{7,3},{8,12},{9,13},{10,... | collective-permute-start | bytes 12296 | tf_op jit(solution)/shard_map/ppermute | solution.py:124
  200.4 15.7 %collective-permute-start.6 = (f32[128,2,8]{0,1,2:T(2,128)S(1)}, f32[128,2,8]{0,1,2:T(2,128)S(1)}, u32[]{:S(2)}, u32[]{:S(2)}) collective-permute-start(f32[128,2,8]{0,1,2:T(2,128)S(1)} %maximum_select_fusion.3), channel_id=1, source_target_pairs={{0,8},{1,9},{2,10},{3,11},{4,12},{5,13},{6,14},{7,15},{8,0},{9,1},... | collective-permute-start | bytes 24584 | tf_op jit(solution)/shard_map/ppermute | solution.py:124
  203.0 13.7 %copy-start = (s32[2]{0:T(128)S(1)}, s32[2]{0:T(128)}, u32[]{:S(2)}) copy-start(s32[2]{0:T(128)} %param.4) | copy-start | bytes 28
Sparse Core Ops, SparseCore 0:
  56.7 88.4 reduce-scatter.2
  216.2 29.2 reduce-scatter.4

commit v11 on v5

--- a/solution.py
+++ b/solution.py
@@ -115,16 +115,20 @@
     feed_index = (2 * window_stations[:, None] + jnp.arange(2, dtype=jnp.int32)[None, :]).reshape(
         -1
     )
-    selector = (
+    onehot = (
         jnp.arange(inputs, dtype=jnp.int32)[:, None] == feed_index[None, :]
+    ).astype(jnp.float32)
+    zero = jnp.zeros_like(onehot)
+    selector = jnp.stack(
+        [
+            jnp.stack([jnp.stack([onehot, zero], 1), jnp.stack([zero, -onehot], 1)], 1),
+            jnp.stack([jnp.stack([zero, onehot], 1), jnp.stack([onehot, zero], 1)], 1),
+        ],
+        0,
+    ).reshape(2, inputs, 2, -1).astype(voltages.dtype)
+    left = jnp.einsum(
+        "tcsi,sirq->tcrq", voltages, selector, preferred_element_type=jnp.float32
     ).astype(voltages.dtype)
-    picked = jnp.einsum(
-        "tcri,iw->tcrw", voltages, selector, preferred_element_type=jnp.float32
-    ).astype(voltages.dtype)
-    left = jnp.stack(
-        [picked, jnp.stack([picked[:, :, 1], -picked[:, :, 0]], 2)], 3
-    )
-    left = left.reshape(*picked.shape[:3], -1)
     partial = jnp.einsum(
         "tcrq,tcri->iqc", left, voltages, preferred_element_type=jnp.float32
     ).astype(jnp.bfloat16)

time: 237 us -> 237 us (level)
    convert_element_type x0 -> x1, local copies, waits for them, and re-layouts: none -> 4.79 us  [per_device(): left = jnp.einsum('tcsi,sirq->tcrq', voltages, selector, preferred_elemen...]
    reshape x1 -> x0, local copies, waits for them, and re-layouts: 4.72 us -> none  [per_device(): left = left.reshape(*picked.shape[:3], -1)]
where the time goes in v11:
time: 237 us; the launch traced here: 236 us
  waiting for transfers between devices  82.9 us (35%)
  matrix products  41.3 us (17%)
  other arithmetic  37.9 us (16%)
  blocking collectives  36.5 us (15%)
  local copies, waits for them, and re-layouts  22.9 us (10%)
  between operations  14.3 us (6%)
    reduce_scatter x1, waiting for transfers between devices, per_device(): lax.psum_scatter(partial, 'tm', scatter_dimension=0, tiled=True)  56.5 us
    reduce_scatter x1, waiting for transfers between devices, per_device(): lax.psum_scatter(spectrum.reshape(block_pairs // 2, -1, DEPTH), 'chan', s...  26.4 us
    all_gather x1, blocking collectives, per_device(): lax.all_gather(lax.psum(baseline_stats, 'chan'), 'tm', axis=0, tiled=True)  23 us
    dot_general x1, matrix products, per_device(): jnp.einsum('tcrq,tcri->iqc', left, voltages, preferred_element_type=jnp.f...  19.2 us
    convert_element_type x1, other arithmetic, phase_table(): jnp.sin(angles).astype(jnp.bfloat16)  17 us
    neg x1, other arithmetic, add_block(): -sine_part  14.4 us
    convert_element_type x1, local copies, waits for them, and re-layouts, per_device(): partial = jnp.einsum('tcrq,tcri->iqc', left, voltages, preferred_element_...  13.6 us
    psum x1, blocking collectives, per_device(): lax.psum(baseline_stats, 'chan')  13.5 us
  transfers between devices with their start and end apart: 2, of which 2 were waited for; matrix products, arithmetic and copies ran while one was open for 14% of the time, Pallas kernels for 0%

profile of v11, /device:TPU:0, one launch (start us, length us, event | category | flops | bytes accessed | tf_op | source)
XLA Modules:
  0.0 236.0 jit_solution(5194886525933203208)
XLA Ops:
  7.2 0.7 broadcast_multiply_fusion.3
  8.3 9.7 %fusion.24 = bf16[8,1024,2,8]{1,3,0,2:T(8,128)(2,1)S(1)} fusion(bf16[8,1024,2,512]{3,2,1,0:T(2,128)(2,1)} %param.3, bf16[1,512,1,8]{1,3,0,2:T(8,128)(2,1)S(1)} %bitcast.199, bf16[1,512,1,8]{1,3,0,2:T(8,128)(2,1)S(1)} %bitcast.200, bf16[1,512,1,8]{1,3,0,2:T(8,128)(2,1)S(1)} %bitcast.201), kind=kOutput, calls=%fused_computation.21 | convolution fusion | flops 268697600 | bytes 17063936 | tf_op jit(solution)/shard_map/tcsi,sirq->tcrq/dot_general | solution.py:129
  18.0 4.8 %copy.131 = bf16[8,1024,2,8]{0,3,2,1:T(8,128)(2,1)} copy(bf16[8,1024,2,8]{1,3,0,2:T(8,128)(2,1)S(1)} %fusion.24) | data formatting | bytes 524288 | tf_op jit(solution)/shard_map/convert_element_type | solution.py:131
  22.7 19.2 %fusion.5 = bf16[512,8,1024]{0,1,2:T(8,128)(2,1)} fusion(bf16[8,1024,2,8]{0,3,2,1:T(8,128)(2,1)} %copy.131, bf16[8,1024,2,512]{3,2,1,0:T(2,128)(2,1)} %param.3), kind=kOutput, calls=%fused_computation.6 | convolution fusion | flops 138412032 | bytes 25427968 | tf_op jit(solution)/shard_map/tcrq,tcri->iqc/dot_general | solution.py:132
  41.9 13.6 %copy.133 = bf16[512,8,1024]{2,1,0:T(8,128)(2,1)} copy(bf16[512,8,1024]{0,1,2:T(8,128)(2,1)} %fusion.5) | data formatting | bytes 16777216 | tf_op jit(solution)/shard_map/convert_element_type | solution.py:134
  55.6 0.2 reduce-scatter.5.cloned.1.call-start
  55.8 0.7 broadcast_multiply_fusion.2
  56.5 14.4 %fusion.27 = bf16[1024,1024]{1,0:T(8,128)(2,1)S(1)} fusion(f32[1024]{0:T(1024)S(1)} %get-tuple-element.82, f32[1024]{0:T(1024)S(1)} %get-tuple-element.83), kind=kLoop, calls=%fused_computation.22 | loop fusion | flops 5242880 | bytes 2105344 | tf_op jit(solution)/shard_map/while/body/eval_jaxpr/neg | solution.py:95
  70.9 17.0 %fusion.17 = (bf16[1024,1024]{1,0:T(8,128)(2,1)}, bf16[1024,1024]{1,0:T(8,128)(2,1)}) fusion(f32[1024]{0:T(1024)S(1)} %get-tuple-element.82, f32[1024]{0:T(1024)S(1)} %get-tuple-element.83), kind=kLoop, calls=%fused_computation.18 | loop fusion | flops 3145728 | bytes 4202496 | tf_op jit(solution)/shard_map/while/body/eval_jaxpr/convert_element_type | solution.py:19
  88.0 56.5 %reduce-scatter.3.cloned.1.call-done = bf16[32,8,1024]{2,1,0:T(8,128)(2,1)} async-done(((bf16[512,8,1024]{2,1,0:T(8,128)(2,1)}), bf16[32,8,1024]{2,1,0:T(8,128)(2,1)}) %reduce-scatter.3.cloned.1.call-update) | async-done | bytes 524304 | tf_op jit(solution)/shard_map/reduce_scatter | solution.py:136
  144.5 1.2 reshape_reshape.6
  145.7 1.1 fusion.56
  147.0 0.3 fusion.35
  147.3 0.3 fusion.40
  147.7 13.5 %psum.7 = f32[16,2,8]{0,1,2:T(2,128)S(1)} all-reduce(f32[16,2,8]{0,1,2:T(2,128)S(1)} %constant_dynamic-update-slice_fusion), channel_id=1, replica_groups=mesh['chan'=8,'tm'=16] {'chan'}, use_global_device_ids=true, to_apply=%region_10.0 | all-reduce | flops 256 | bytes 2048 | tf_op jit(solution)/shard_map/psum | solution.py:158
  161.3 23.0 %all_gather.3 = f32[256,2,8]{2,1,0:T(2,128)S(1)} all-gather(f32[16,2,8]{2,1,0:T(2,128)S(1)} %copy.156), channel_id=1, replica_groups=mesh['chan'=8,'tm'=16] {'tm'}, dimensions={0}, use_global_device_ids=true | all-gather | bytes 17408 | tf_op jit(solution)/shard_map/all_gather | solution.py:157
  185.3 0.2 select_reduce_fusion.17
  186.2 0.2 select_reduce_fusion.13
  187.5 12.4 %fusion.6 = f32[32,2048]{1,0:T(8,128)S(1)} fusion(bf16[1024,1024]{1,0:T(8,128)(2,1)} %get-tuple-element.75, bf16[1024,1024]{1,0:T(8,128)(2,1)} %get-tuple-element.74, bf16[1024,1024]{1,0:T(8,128)(2,1)S(1)} %fusion.27, bf16[32,1024]{1,0:T(8,128)(2,1)S(1)} %multiply_convert_fusion, bf16[32,1024]{1,0:T(8,128)(2,1)S(1)} %multiply_convert_fusion.1), kind=kOutput, calls=%fused_computation.7 | convolution fusion | flops 302252032 | bytes 6684672 | tf_op jit(solution)/shard_map/while/body/eval_jaxpr/dot_general | solution.py:97
  199.9 0.7 reshape_reshape.7
  200.8 0.6 pad_maximum_fusion
  201.4 26.4 %reduce-scatter.5.cloned.1.call-done = f32[1,8,1024]{2,1,0:T(8,128)} async-done(((f32[8,8,1024]{2,1,0:T(8,128)}), f32[1,8,1024]{2,1,0:T(8,128)}) %reduce-scatter.5.cloned.1.call-update) | async-done | bytes 32784 | tf_op jit(solution)/shard_map/reduce_scatter | solution.py:152
  227.8 0.8 broadcast_multiply_fusion
  228.6 0.6 reshape.292
  (61 shorter events, 3.7 us)
Async XLA Ops:
  7.2 137.3 %reduce-scatter.3.cloned.1.call-start = ((), (), s32[]{:S(2)}) async-start(), calls=%async_computation.2 | async-start | bytes 8912896 | tf_op jit(solution)/shard_map/reduce_scatter | solution.py:136
  55.6 172.2 %reduce-scatter.5.cloned.1.call-start = ((), (), s32[]{:S(2)}) async-start(), calls=%async_computation.3 | async-start | bytes 294912 | tf_op jit(solution)/shard_map/reduce_scatter | solution.py:152
  70.9 114.1 %copy-start = (s32[2]{0:T(128)S(1)}, s32[2]{0:T(128)}, u32[]{:S(2)}) copy-start(s32[2]{0:T(128)} %param.4) | copy-start | bytes 28
Sparse Core Ops, SparseCore 0:
  55.7 88.7 reduce-scatter.2
  200.7 27.0 reduce-scatter.4

commit v12 on v11

--- a/solution.py
+++ b/solution.py
@@ -3,11 +3,12 @@
 import jax
 import jax.numpy as jnp
 from jax import lax
-from jax.sharding import PartitionSpec as P
+from jax.sharding import Mesh, PartitionSpec as P
 
 CHANNELS = 8192
 DEPTH = 1024
 ITERATIONS = 3
+CHAN = ("chan_outer", "chan_inner")
 
 
 def phase_table(first_channel, channel_count):
@@ -107,7 +108,7 @@
 
 def per_device(voltages, window_stations, channel_flags):
     tm_size = lax.axis_size("tm")
-    chan_size = lax.axis_size("chan")
+    chan_size = lax.axis_size(CHAN)
     inputs = voltages.shape[3]
     stations = inputs // 2
     window = window_stations.shape[0]
@@ -139,7 +140,7 @@
         scatter_dimension=0,
         tiled=True,
     ).reshape(-1, *partial_shape[1:])
-    chan_index = lax.axis_index("chan")
+    chan_index = lax.axis_index(CHAN)
     tm_index = lax.axis_index("tm")
     first_channel = chan_index * channel_count
     local_flags = lax.dynamic_slice_in_dim(channel_flags, first_channel, channel_count, 0)
@@ -149,13 +150,16 @@
     block_pairs = spectrum.shape[0]
     total_time = voltages.shape[0] * tm_size
     norm_factor = 1.0 / math.sqrt(CHANNELS * total_time)
-    spectrum = lax.psum_scatter(
-        spectrum.reshape(block_pairs // 2, -1, DEPTH), "chan", scatter_dimension=0, tiled=True
-    )
+    outer = lax.axis_size("chan_outer")
+    inner = lax.axis_size("chan_inner")
+    spectrum = spectrum.reshape(outer, inner, -1, DEPTH)
+    spectrum = jnp.swapaxes(spectrum, 0, 1).reshape(outer * inner, -1, DEPTH)
+    spectrum = lax.psum_scatter(spectrum, "chan_inner", scatter_dimension=0, tiled=True)
+    spectrum = lax.psum_scatter(spectrum, "chan_outer", scatter_dimension=0, tiled=True)
     own_pairs = block_pairs // chan_size
     rm_spectrum = (spectrum * norm_factor).reshape(1, own_pairs, window, 2, DEPTH)
     all_stats = lax.all_gather(
-        lax.psum(baseline_stats, "chan"), "tm", axis=0, tiled=True
+        lax.psum(baseline_stats, CHAN), "tm", axis=0, tiled=True
     ) / CHANNELS
     station_axis = jnp.arange(stations, dtype=jnp.int32)
     window_map = (window_stations[:, None] == station_axis[None, :]).astype(jnp.float32)
@@ -173,10 +177,16 @@
 
 
 def solution(mesh):
+    chan_size, tm_size = mesh.devices.shape
+    inner = 2 if chan_size % 2 == 0 else 1
+    split_mesh = Mesh(
+        mesh.devices.reshape(chan_size // inner, inner, tm_size),
+        ("chan_outer", "chan_inner", "tm"),
+    )
     return jax.shard_map(
         per_device,
-        mesh=mesh,
-        in_specs=(P("tm", "chan", None, None), P(), P()),
-        out_specs=(P("tm", "chan", None, None, None), P()),
+        mesh=split_mesh,
+        in_specs=(P("tm", CHAN, None, None), P(), P()),
+        out_specs=(P("tm", CHAN, None, None, None), P()),
         check_vma=False,
     )

time: 237 us -> 240 us (1.013)
  waiting for transfers between devices: 82.9 us -> 86.2 us
    reduce_scatter x1 -> x2, waiting for transfers between devices: 26.4 us -> 29.7 us  [the longest x1 23.8 us: per_device(): lax.psum_scatter(spectrum, 'chan_outer', scatter_dimension=0, tiled=True)]
  transfers between devices with their start and end apart: 2 -> 3, of which waited for: 2 -> 3; matrix products, arithmetic and copies ran while one was open for 14% -> 14% of each run, Pallas kernels for 0% -> 0%
where the time goes in v12:
time: 240 us; the launch traced here: 239 us
  waiting for transfers between devices  86.2 us (36%)
  matrix products  41.3 us (17%)
  other arithmetic  37.9 us (16%)
  blocking collectives  36.5 us (15%)
  local copies, waits for them, and re-layouts  22.9 us (10%)
  between operations  14 us (6%)
    reduce_scatter x1, waiting for transfers between devices, per_device(): lax.psum_scatter(partial, 'tm', scatter_dimension=0, tiled=True)  56.5 us
    reduce_scatter x1, waiting for transfers between devices, per_device(): lax.psum_scatter(spectrum, 'chan_outer', scatter_dimension=0, tiled=True)  23.8 us
    all_gather x1, blocking collectives, per_device(): lax.all_gather(lax.psum(baseline_stats, CHAN), 'tm', axis=0, tiled=True)  23 us
    dot_general x1, matrix products, per_device(): jnp.einsum('tcrq,tcri->iqc', left, voltages, preferred_element_type=jnp.f...  19.2 us
    convert_element_type x1, other arithmetic, phase_table(): jnp.sin(angles).astype(jnp.bfloat16)  17 us
    neg x1, other arithmetic, add_block(): -sine_part  14.4 us
    convert_element_type x1, local copies, waits for them, and re-layouts, per_device(): partial = jnp.einsum('tcrq,tcri->iqc', left, voltages, preferred_element_...  13.6 us
    psum x1, blocking collectives, per_device(): lax.psum(baseline_stats, CHAN)  13.4 us
  transfers between devices with their start and end apart: 3, of which 3 were waited for; matrix products, arithmetic and copies ran while one was open for 14% of the time, Pallas kernels for 0%

profile of v12, /device:TPU:0, one launch (start us, length us, event | category | flops | bytes accessed | tf_op | source)
XLA Modules:
  0.0 239.1 jit_solution(14443196220314387761)
XLA Ops:
  7.2 0.7 broadcast_multiply_fusion.3
  8.3 9.7 %fusion.24 = bf16[8,1024,2,8]{1,3,0,2:T(8,128)(2,1)S(1)} fusion(bf16[8,1024,2,512]{3,2,1,0:T(2,128)(2,1)} %param.3, bf16[1,512,1,8]{1,3,0,2:T(8,128)(2,1)S(1)} %bitcast.203, bf16[1,512,1,8]{1,3,0,2:T(8,128)(2,1)S(1)} %bitcast.204, bf16[1,512,1,8]{1,3,0,2:T(8,128)(2,1)S(1)} %bitcast.205), kind=kOutput, calls=%fused_computation.21 | convolution fusion | flops 268697600 | bytes 17063936 | tf_op jit(solution)/shard_map/tcsi,sirq->tcrq/dot_general | solution.py:130
  18.0 4.8 %copy.135 = bf16[8,1024,2,8]{0,3,2,1:T(8,128)(2,1)} copy(bf16[8,1024,2,8]{1,3,0,2:T(8,128)(2,1)S(1)} %fusion.24) | data formatting | bytes 524288 | tf_op jit(solution)/shard_map/convert_element_type | solution.py:132
  22.7 19.2 %fusion.5 = bf16[512,8,1024]{0,1,2:T(8,128)(2,1)} fusion(bf16[8,1024,2,8]{0,3,2,1:T(8,128)(2,1)} %copy.135, bf16[8,1024,2,512]{3,2,1,0:T(2,128)(2,1)} %param.3), kind=kOutput, calls=%fused_computation.6 | convolution fusion | flops 138412032 | bytes 25427968 | tf_op jit(solution)/shard_map/tcrq,tcri->iqc/dot_general | solution.py:133
  41.9 13.6 %copy.137 = bf16[512,8,1024]{2,1,0:T(8,128)(2,1)} copy(bf16[512,8,1024]{0,1,2:T(8,128)(2,1)} %fusion.5) | data formatting | bytes 16777216 | tf_op jit(solution)/shard_map/convert_element_type | solution.py:135
  55.6 0.2 reduce-scatter.6.cloned.1.call-start
  55.8 0.7 broadcast_multiply_fusion.2
  56.5 14.4 %fusion.27 = bf16[1024,1024]{1,0:T(8,128)(2,1)S(1)} fusion(f32[1024]{0:T(1024)S(1)} %get-tuple-element.82, f32[1024]{0:T(1024)S(1)} %get-tuple-element.83), kind=kLoop, calls=%fused_computation.22 | loop fusion | flops 5242880 | bytes 2105344 | tf_op jit(solution)/shard_map/while/body/eval_jaxpr/neg | solution.py:96
  70.9 17.0 %fusion.17 = (bf16[1024,1024]{1,0:T(8,128)(2,1)}, bf16[1024,1024]{1,0:T(8,128)(2,1)}) fusion(f32[1024]{0:T(1024)S(1)} %get-tuple-element.82, f32[1024]{0:T(1024)S(1)} %get-tuple-element.83), kind=kLoop, calls=%fused_computation.18 | loop fusion | flops 3145728 | bytes 4202496 | tf_op jit(solution)/shard_map/while/body/eval_jaxpr/convert_element_type | solution.py:20
  88.0 56.5 %reduce-scatter.4.cloned.1.call-done = bf16[32,8,1024]{2,1,0:T(8,128)(2,1)} async-done(((bf16[512,8,1024]{2,1,0:T(8,128)(2,1)}), bf16[32,8,1024]{2,1,0:T(8,128)(2,1)}) %reduce-scatter.4.cloned.1.call-update) | async-done | bytes 524304 | tf_op jit(solution)/shard_map/reduce_scatter | solution.py:137
  144.4 1.2 reshape_reshape.6
  145.7 1.1 fusion.56
  147.0 0.3 fusion.35
  147.3 0.3 fusion.40
  147.6 13.4 %psum.7 = f32[16,2,8]{0,1,2:T(2,128)S(1)} all-reduce(f32[16,2,8]{0,1,2:T(2,128)S(1)} %constant_dynamic-update-slice_fusion), channel_id=1, replica_groups=mesh['chan_outer'=4,'chan_inner'=2,'tm'=16] {'chan_outer','chan_inner'}, use_global_device_ids=true, to_apply=%region_11.0 | all-reduce | flops 256 | bytes 2048 | tf_op jit(solution)/shard_map/psum | solution.py:162
  161.2 23.0 %all_gather.3 = f32[256,2,8]{2,1,0:T(2,128)S(1)} all-gather(f32[16,2,8]{2,1,0:T(2,128)S(1)} %copy.161), channel_id=1, replica_groups=mesh['chan_outer'=4,'chan_inner'=2,'tm'=16] {'tm'}, dimensions={0}, use_global_device_ids=true | all-gather | bytes 17408 | tf_op jit(solution)/shard_map/all_gather | solution.py:161
  187.0 12.4 %fusion.6 = f32[32,2048]{1,0:T(8,128)S(1)} fusion(bf16[1024,1024]{1,0:T(8,128)(2,1)} %get-tuple-element.75, bf16[1024,1024]{1,0:T(8,128)(2,1)} %get-tuple-element.74, bf16[1024,1024]{1,0:T(8,128)(2,1)S(1)} %fusion.27, bf16[32,1024]{1,0:T(8,128)(2,1)S(1)} %multiply_convert_fusion, bf16[32,1024]{1,0:T(8,128)(2,1)S(1)} %multiply_convert_fusion.1), kind=kOutput, calls=%fused_computation.7 | convolution fusion | flops 302252032 | bytes 6684672 | tf_op jit(solution)/shard_map/while/body/eval_jaxpr/dot_general | solution.py:98
  199.4 0.7 copy.144
  200.2 0.2 select_reduce_fusion.13
  200.8 5.9 %reduce-scatter.6.cloned.1.call-done = f32[4,8,1024]{2,1,0:T(8,128)} async-done(((f32[8,8,1024]{2,1,0:T(8,128)}), f32[4,8,1024]{2,1,0:T(8,128)}) %reduce-scatter.6.cloned.1.call-update) | async-done | bytes 131088 | tf_op jit(solution)/shard_map/reduce_scatter | solution.py:157
  206.8 0.6 pad_maximum_fusion
  207.4 23.8 %reduce-scatter.8.cloned.1.call-done = f32[1,8,1024]{2,1,0:T(8,128)} async-done(((f32[4,8,1024]{2,1,0:T(8,128)}), f32[1,8,1024]{2,1,0:T(8,128)}) %reduce-scatter.8.cloned.1.call-update) | async-done | bytes 32784 | tf_op jit(solution)/shard_map/reduce_scatter | solution.py:158
  231.2 0.8 broadcast_multiply_fusion
  232.0 0.6 reshape.296
  (65 shorter events, 4.0 us)
Async XLA Ops:
  7.2 137.3 %reduce-scatter.4.cloned.1.call-start = ((), (), s32[]{:S(2)}) async-start(), calls=%async_computation.3 | async-start | bytes 8912896 | tf_op jit(solution)/shard_map/reduce_scatter | solution.py:137
  55.6 151.2 %reduce-scatter.6.cloned.1.call-start = ((), (), s32[]{:S(2)}) async-start(), calls=%async_computation.4 | async-start | bytes 393216 | tf_op jit(solution)/shard_map/reduce_scatter | solution.py:157
  70.9 114.1 %copy-start = (s32[2]{0:T(128)S(1)}, s32[2]{0:T(128)}, u32[]{:S(2)}) copy-start(s32[2]{0:T(128)} %param.4) | copy-start | bytes 28
  200.1 31.1 %reduce-scatter.8.cloned.1.call-start = ((), (), s32[]{:S(2)}) async-start(), calls=%async_computation.5 | async-start | bytes 163840 | tf_op jit(solution)/shard_map/reduce_scatter | solution.py:158
Sparse Core Ops, SparseCore 0:
  55.7 88.6 reduce-scatter.3
  200.2 6.4 reduce-scatter.5
  209.1 22.0 reduce-scatter.7
